TPU v7x, 512 devices: a whole 4x8x8 slice. The times are simulated.
512 devices in a mesh: gx: 8 (over y), gy: 64 (over z, x, core).
Axes of the slice: x: 4, y: 8, z: 8, core: 2. Of those that a mesh axis runs over, the one named last changes fastest.
Arguments:
- source: float32 [512, 256, 128], P('gy', 'gx'), may hold values from -0.004 to 0.004
- mask: int32 [512, 256, 128], P('gy', 'gx'), may hold values from 0 to 2, as said below
- cond_x: float32 [512, 256, 128], P('gy', 'gx'), may hold values from 0.0012 to 0.06
- cond_y: float32 [512, 256, 128], P('gy', 'gx'), may hold values from 0.4 to 5
- cond_z: float32 [512, 256, 128], P('gy', 'gx'), may hold values from 0.0004 to 0.01
Outputs:
- solution: float32 [512, 256, 128], P('gy', 'gx')
Inputs may be any that keep to these rules, and one draw needn't show every extreme that they name: `mask`: 0 marks a fluid cell, 1 a cut cell, 2 a solid cell.
All inputs are finite; a program needn't handle non-finite values.
Results may differ from a plain program's by a relative error of at most 0.00095.
Values sent between devices are 32-bit elements; how exact they have to be, the bound alone decides.
No kernel may reach another device: no remote copies, remote signals or barrier semaphores. Data moves between devices by JAX's collectives and lax.ppermute only.
A program may use at most 128 MiB of HBM per device.

v0:
```python
import jax
import jax.numpy as jnp
from jax import lax
from jax.sharding import Mesh
from jax.sharding import PartitionSpec as P

LEVELS = 6
GY = ("gy_0", "gy_1", "gy_2")


base_shift = 0.001
wall_term = 0.02


def in_blocks(x, dim, count):
    before, after = (x.shape[:dim], x.shape[dim + 1 :])
    return jnp.moveaxis(x.reshape(*before, count, -1, *after), dim, 0)


def in_order(parts, dim):
    parts = jnp.moveaxis(parts, 0, dim)
    shape = parts.shape
    return parts.reshape(*shape[:dim], shape[dim] * shape[dim + 1], *shape[dim + 2 :])


def turned_blocks(parts, axes, sequence):
    shape = [lax.axis_size(a) for a in axes]
    parts = parts.reshape(*shape, *parts.shape[1:])
    for k in sequence:
        parts = lax.all_to_all(parts, axes[k], split_axis=k, concat_axis=k, tiled=True)
    return parts.reshape(-1, *parts.shape[len(axes) :])


def exchange_by_chip(x, groups, sequence, split_dim, concat_dim):
    count = lax.axis_size(groups[0]) * lax.axis_size(groups[1])
    parts = in_blocks(x, split_dim, count)
    return in_order(turned_blocks(parts, groups, sequence), concat_dim)


def copy_for_each(x, axis):
    count = lax.axis_size(axis)
    return lax.all_to_all(jnp.broadcast_to(x[None], (count, *x.shape)), axis, 0, 0, tiled=True)


def gather_directly(x, axis, dim):
    parts = copy_for_each(x, axis)
    return in_order(parts, dim)


def padded(cells, sides, width):
    for axis, dim in sides:
        count = lax.axis_size(axis)
        ends = count - 1
        head = lax.slice_in_dim(cells, 0, width, axis=dim)
        tail = lax.slice_in_dim(cells, cells.shape[dim] - width, cells.shape[dim], axis=dim)
        cells = jnp.concatenate(
            [
                lax.ppermute(tail, axis, [(i, (i + 1) % count) for i in range(ends)]),
                cells,
                lax.ppermute(head, axis, [((i + 1) % count, i) for i in range(ends)]),
            ],
            axis=dim,
        )
    return cells


def with_halo(x, sides, width):
    edges = {}
    for axis, dim in sides:
        count, length = (lax.axis_size(axis), x.shape[dim])
        up = [(i, (i + 1) % count) for i in range(count - 1)]
        last = lax.slice_in_dim(x, length - width, length, axis=dim)
        leading = lax.slice_in_dim(x, 0, width, axis=dim)
        edges[dim] = (
            lax.ppermute(last, axis, up),
            lax.ppermute(leading, axis, [(b, a) for a, b in up]),
        )
    done = []
    for _, dim in sides:
        low, high = edges[dim]
        around = [(width, width) if d in done else (0, 0) for d in range(x.ndim)]
        x = jnp.concatenate([jnp.pad(low, around), x, jnp.pad(high, around)], axis=dim)
        done.append(dim)
    return x


def swapped(x, axis, stride):
    return lax.ppermute(x, axis, [(i, i ^ 1 << stride) for i in range(lax.axis_size(axis))])


def ahead(field, axis):
    size = field.shape[axis]
    edge = jnp.zeros_like(lax.slice_in_dim(field, 0, 1, axis=axis))
    return jnp.concatenate([lax.slice_in_dim(field, 1, size, axis=axis), edge], axis=axis)


def behind(field, axis):
    size = field.shape[axis]
    edge = jnp.zeros_like(lax.slice_in_dim(field, 0, 1, axis=axis))
    return jnp.concatenate([edge, lax.slice_in_dim(field, 0, size - 1, axis=axis)], axis=axis)


def coarse_sum(field):
    depth, width, height = field.shape
    return field.reshape(depth // 2, 2, width // 2, 2, height // 2, 2).sum(axis=(1, 3, 5))


def coarse_face(face, axis, parity):
    picked = lax.slice_in_dim(face, parity, face.shape[axis], stride=2, axis=axis)
    return 0.125 * coarse_sum(jnp.repeat(picked, 2, axis=axis))


def prolong(field):
    return jnp.repeat(jnp.repeat(jnp.repeat(field, 2, axis=0), 2, axis=1), 2, axis=2)


def upper_flag(bit):
    return lax.axis_index(GY) // 2**bit % 2


def line_factors(lower, diag, upper):
    denoms = [diag[0]]
    ratios = [upper[0] / diag[0]]
    for place in range(1, diag.shape[0]):
        pivot = diag[place] - lower[place] * ratios[place - 1]
        denoms.append(pivot)
        ratios.append(upper[place] / pivot)
    return (denoms, ratios)


def rows_solve(level, rhs):
    lower = level["lower"]
    denoms = level["denoms"]
    ratios = level["ratios"]
    count = rhs.shape[0]
    values = [rhs[0] / denoms[0]]
    for place in range(1, count):
        values.append((rhs[place] - lower[place] * values[place - 1]) / denoms[place])
    result = [values[count - 1]]
    for place in range(count - 2, -1, -1):
        result.append(values[place] - ratios[place] * result[-1])
    return jnp.stack(result[::-1])


def assemble(faces, group):
    face_x, low_x, face_y, low_y, face_z, shift = faces
    low_z = behind(face_z, 2)
    diag = shift + face_x + low_x + face_y + low_y + face_z + low_z
    level = {
        "face_x": face_x,
        "low_x": low_x,
        "face_y": face_y,
        "low_y": low_y,
        "face_z": face_z,
        "low_z": low_z,
        "diag": diag,
        "group": group,
    }
    level["lower"] = -low_y
    denoms, ratios = line_factors(-low_y, diag, -face_y)
    level["denoms"] = denoms
    level["ratios"] = ratios
    blank = jnp.zeros_like(diag)
    level["first_resp"] = rows_solve(level, blank.at[0].set(1.0))
    level["last_resp"] = rows_solve(level, blank.at[-1].set(1.0))
    level["alpha"] = low_y[0] * level["first_resp"][0]
    level["gamma"] = low_y[0] * level["first_resp"][-1]
    level["beta"] = face_y[-1] * level["last_resp"][0]
    level["delta"] = face_y[-1] * level["last_resp"][-1]
    return level


def forward_terms(alpha, beta, gamma, delta, head, tail):
    zeros = jnp.zeros_like(head)
    ones = jnp.ones_like(head)
    return (
        gamma * beta - alpha * delta,
        zeros,
        delta,
        gamma * head - alpha * tail,
        gamma,
        tail,
        -alpha,
        zeros,
        ones,
    )


def chain_forward(earlier, later):
    product = []
    for left_row in range(3):
        for column in range(3):
            product.append(
                later[3 * left_row] * earlier[column]
                + later[3 * left_row + 1] * earlier[3 + column]
                + later[3 * left_row + 2] * earlier[6 + column]
            )
    scale = product[8]
    return tuple((entry / scale for entry in product))


def chain_backward(earlier, later):
    return (later[0] + later[1] * earlier[0], later[1] * earlier[1])


def settle(alpha, beta, head, state):
    carry_q = state[2] / state[8]
    carry_p = state[5] / state[8]
    pivot = 1.0 - alpha * carry_q
    return ((head + alpha * carry_p) / pivot, beta / pivot, carry_q, carry_p)


def reduced_local(alpha, beta, gamma, delta, head, tail):
    zeros = jnp.zeros_like(head[:1])
    ones = jnp.ones_like(head[:1])
    identity = (ones, zeros, zeros, zeros, ones, zeros, zeros, zeros, ones)
    terms = forward_terms(alpha, beta, gamma, delta, head, tail)
    inclusive = lax.associative_scan(chain_forward, terms, axis=0)
    state = tuple(
        (jnp.concatenate([plain, entry[:-1]], axis=0) for plain, entry in zip(identity, inclusive))
    )
    start, slope, carry_q, carry_p = settle(alpha, beta, head, state)
    later = lax.associative_scan(chain_backward, (start, slope), reverse=True, axis=0)
    next_first = jnp.concatenate([later[0][1:], zeros], axis=0)
    first = start + slope * next_first
    return (carry_p + carry_q * first, next_first)


def pick_block(values, index, shape):
    return lax.dynamic_index_in_dim(values, index, 0, keepdims=False).reshape(shape)


def reduced_moved(level, head, tail):
    group = level["group"]
    shape = head.shape
    packed = jnp.stack(
        [level["alpha"], level["beta"], level["gamma"], level["delta"], head, tail]
    ).reshape(6, 1, -1)
    if group == 1:
        moved = exchange_by_chip(packed, (("gy_0", "gy_1"), "gy_2"), (1, 0), 2, 1)
        prev_last, next_first = reduced_local(
            moved[0], moved[1], moved[2], moved[3], moved[4], moved[5]
        )
        back = lax.all_to_all(
            jnp.stack([prev_last, next_first]), GY, split_axis=1, concat_axis=2, tiled=True
        )
        return (back[0, 0].reshape(shape), back[1, 0].reshape(shape))
    whole = gather_directly(packed, GY, 1)
    whole = whole.reshape(6, whole.shape[1] // group, group, -1)[:, :, 0]
    prev_last, next_first = reduced_local(
        whole[0], whole[1], whole[2], whole[3], whole[4], whole[5]
    )
    index = lax.axis_index(GY) // group
    return (pick_block(prev_last, index, shape), pick_block(next_first, index, shape))


def line_solve(level, rhs):
    local = rows_solve(level, rhs)
    prev_last, next_first = reduced_moved(level, local[0], local[-1])
    return (
        local
        + (level["low_y"][0] * prev_last)[None] * level["first_resp"]
        + (level["face_y"][-1] * next_first)[None] * level["last_resp"]
    )


def neighbour_terms(level, field):
    rim = padded(field, (("gx", 1),), 1)
    return (
        level["face_x"] * rim[:, 2:]
        + level["low_x"] * rim[:, :-2]
        + level["face_z"] * ahead(field, 2)
        + level["low_z"] * behind(field, 2)
    )


def relax(level, field, rhs):
    return line_solve(level, rhs + neighbour_terms(level, field))


def body(source, mask, cond_x, cond_y, cond_z):
    open_cells = (mask != 2).astype(jnp.float32)
    wall = (mask == 1).astype(jnp.float32)
    rim = with_halo(
        jnp.stack([cond_x * open_cells, cond_y * open_cells, open_cells]), (("gx", 2), (GY, 1)), 1
    )
    faces = (
        cond_x * open_cells * rim[2, 1:-1, 2:],
        rim[0, 1:-1, :-2] * open_cells,
        cond_y * open_cells * rim[2, 2:, 1:-1],
        rim[1, :-2, 1:-1] * open_cells,
        cond_z * open_cells * ahead(open_cells, 2),
        base_shift + wall_term * wall,
    )
    rhs = source * open_cells
    levels = []
    fields = []
    sources = []
    residual = rhs
    for depth in range(LEVELS):
        group = 1
        if depth > 0:
            face_x, low_x, face_y, low_y, face_z, shift = faces
            faces = (
                coarse_face(face_x, 1, 1),
                coarse_face(low_x, 1, 0),
                coarse_face(face_y, 0, 1),
                coarse_face(low_y, 0, 0),
                coarse_face(face_z, 2, 1),
                0.25 * coarse_sum(shift),
            )
            rhs = 0.25 * coarse_sum(residual)
            if depth >= 2:
                group = 2 ** (depth - 1)
                stacked = jnp.stack((rhs,) + faces)
                partner = swapped(stacked, GY, depth - 2)
                upper = upper_flag(depth - 2) == 1
                folded = jnp.concatenate(
                    [jnp.where(upper, partner, stacked), jnp.where(upper, stacked, partner)], axis=1
                )
                rhs = folded[0]
                faces = tuple((folded[place] for place in range(1, 7)))
        level = assemble(faces, group)
        field = line_solve(level, rhs)
        if depth == LEVELS - 1:
            field = relax(level, field, rhs)
        else:
            residual = neighbour_terms(level, field)
        levels.append(level)
        fields.append(field)
        sources.append(rhs)
    correction = fields[-1]
    for depth in range(LEVELS - 2, -1, -1):
        if depth + 1 >= 2:
            half = correction.shape[0] // 2
            correction = lax.dynamic_slice_in_dim(correction, upper_flag(depth - 1) * half, half, 0)
        field = fields[depth] + prolong(correction)
        correction = relax(levels[depth], field, sources[depth])
    return correction


def solution(mesh):
    finer = Mesh(mesh.devices.reshape(mesh.shape["gx"], 8, 4, 2), ("gx", "gy_0", "gy_1", "gy_2"))
    return jax.shard_map(
        body,
        mesh=finer,
        in_specs=(
            P(GY, "gx", None),
            P(GY, "gx", None),
            P(GY, "gx", None),
            P(GY, "gx", None),
            P(GY, "gx", None),
        ),
        out_specs=P(GY, "gx", None),
        check_vma=False,
    )
```

profile of v0, /device:TPU:57, one launch (start us, length us, event | category | flops | bytes accessed | tf_op | source)
XLA Modules:
  0.0 558.8 jit_solution(13831016730573671685)
XLA Ops:
  2.1 3.7 collective-permute-start.3
  5.8 3.0 collective-permute-start
  12.1 9.8 %reshape.2289 = f32[4,2,16,2,64,2]{5,4,3,2,1,0:T(8,128)} reshape(f32[8,32,128]{2,1,0:T(8,128)S(1)} %get-tuple-element.716) | data formatting | bytes 262144 | tf_op jit(solution)/shard_map/reshape | solution.py:105
  21.9 4.6 reduce_sum.331
  28.1 2.9 slice.7986
  32.1 3.5 all_to_all.116
  38.2 14.7 %all-to-all-start.1 = ((f32[32,1,768]{2,1,0:T(1,128)}), f32[32,1,768]{2,1,0:T(1,128)}, u32[]{:S(2)}, u32[]{:S(2)}) async-start(f32[32,1,768]{2,1,0:T(1,128)} %reshape.2437), calls=%async_computation.1 | async-start | bytes 196608 | tf_op jit(solution)/shard_map/all_to_all | solution.py:30
  85.5 10.7 %all-to-all-start.2 = ((f32[64,1,128]{2,1,0:T(1,128)}), f32[64,1,128]{2,1,0:T(1,128)S(1)}, u32[]{:S(2)}, u32[]{:S(2)}) async-start(f32[64,1,128]{2,1,0:T(1,128)} %reshape.2439), calls=%async_computation.2 | async-start | bytes 65536 | tf_op jit(solution)/shard_map/all_to_all | solution.py:244
  96.8 8.8 %all-to-all-done.2 = f32[64,1,128]{2,1,0:T(1,128)S(1)} async-done(((f32[64,1,128]{2,1,0:T(1,128)}), f32[64,1,128]{2,1,0:T(1,128)S(1)}, u32[]{:S(2)}, u32[]{:S(2)}) %all-to-all-start.2) | async-done | bytes 32800 | tf_op jit(solution)/shard_map/all_to_all | solution.py:244
  107.8 4.0 collective-permute-start.4
  113.2 2.9 collective-permute-done.5
  116.3 9.8 %reshape.2288 = f32[4,2,16,2,64,2]{5,4,3,2,1,0:T(8,128)} reshape(f32[8,32,128]{2,1,0:T(8,128)S(1)} %fusion.9) | data formatting | bytes 262144 | tf_op jit(solution)/shard_map/reshape | solution.py:105
  126.1 4.0 reduce_sum.329
  133.2 5.5 all_to_all.117
  140.5 4.3 all-to-all-start.4
  145.8 7.7 %all-to-all-done.4 = f32[32,1,192]{2,1,0:T(1,128)S(1)} async-done(((f32[32,1,192]{2,1,0:T(1,128)}), f32[32,1,192]{2,1,0:T(1,128)S(1)}, u32[]{:S(2)}, u32[]{:S(2)}) %all-to-all-start.4) | async-done | bytes 24608 | tf_op jit(solution)/shard_map/all_to_all | solution.py:30
  159.9 5.5 all-to-all-start.5
  167.4 8.1 %all-to-all-done.5 = f32[2,64,16]{2,0,1:T(2,128)S(1)} async-done(((f32[2,64,16]{2,0,1:T(2,128)}), f32[2,64,16]{2,0,1:T(2,128)S(1)}, u32[]{:S(2)}, u32[]{:S(2)}) %all-to-all-start.5) | async-done | bytes 8224 | tf_op jit(solution)/shard_map/all_to_all | solution.py:244
  176.0 3.0 collective-permute-start.6
  180.4 3.0 collective-permute-done.7
  186.8 3.7 collective-permute-start.8
  193.1 4.4 all-to-all-start.6
  199.2 13.7 %all-to-all-done.6 = f32[64,6,1,256]{3,2,1,0:T(1,128)S(1)} async-done(((f32[64,6,1,256]{3,2,1,0:T(1,128)}), f32[64,6,1,256]{3,2,1,0:T(1,128)S(1)}, u32[]{:S(2)}, u32[]{:S(2)}) %all-to-all-start.6) | async-done | bytes 393248 | tf_op jit(solution)/shard_map/all_to_all | solution.py:42
  219.4 4.5 collective-permute-start.9
  232.6 7.4 %all-to-all-start.7 = ((f32[64,1,384]{2,1,0:T(1,128)}), f32[64,1,384]{2,1,0:T(1,128)S(1)}, u32[]{:S(2)}, u32[]{:S(2)}) async-start(f32[64,1,384]{2,1,0:T(1,128)} %reshape.2445), calls=%async_computation.7 | async-start | bytes 196608 | tf_op jit(solution)/shard_map/all_to_all | solution.py:42
  241.2 9.4 %all-to-all-done.7 = f32[64,1,384]{2,1,0:T(1,128)S(1)} async-done(((f32[64,1,384]{2,1,0:T(1,128)}), f32[64,1,384]{2,1,0:T(1,128)S(1)}, u32[]{:S(2)}, u32[]{:S(2)}) %all-to-all-start.7) | async-done | bytes 98336 | tf_op jit(solution)/shard_map/all_to_all | solution.py:42
  254.8 3.9 collective-permute-start.12
  260.1 3.2 collective-permute-done.13
  263.7 3.0 collective-permute-start.14
  266.7 2.9 collective-permute-done.14
  271.3 6.7 %all-to-all-start.8 = ((f32[64,6,1,16]{3,2,1,0:T(1,128)}), f32[64,6,1,16]{3,2,1,0:T(1,128)S(1)}, u32[]{:S(2)}, u32[]{:S(2)}) async-start(f32[64,6,1,16]{3,2,1,0:T(1,128)} %broadcast_in_dim.306), calls=%async_computation.8 | async-start | bytes 393216 | tf_op jit(solution)/shard_map/all_to_all | solution.py:42
  279.2 11.1 %all-to-all-done.8 = f32[64,6,1,16]{3,2,1,0:T(1,128)S(1)} async-done(((f32[64,6,1,16]{3,2,1,0:T(1,128)}), f32[64,6,1,16]{3,2,1,0:T(1,128)S(1)}, u32[]{:S(2)}, u32[]{:S(2)}) %all-to-all-start.8) | async-done | bytes 24608 | tf_op jit(solution)/shard_map/all_to_all | solution.py:42
  292.6 3.8 collective-permute-start.15
  297.8 4.7 collective-permute-done.16
  308.2 6.7 %all-to-all-start.9 = ((f32[64,6,1,4]{1,3,2,0:T(4,128)}), f32[64,6,1,4]{1,3,2,0:T(4,128)S(1)}, u32[]{:S(2)}, u32[]{:S(2)}) async-start(f32[64,6,1,4]{1,3,2,0:T(4,128)} %broadcast_in_dim.318), calls=%async_computation.9 | async-start | bytes 262144 | tf_op jit(solution)/shard_map/all_to_all | solution.py:42
  315.0 11.3 %all-to-all-done.9 = f32[64,6,1,4]{1,3,2,0:T(4,128)S(1)} async-done(((f32[64,6,1,4]{1,3,2,0:T(4,128)}), f32[64,6,1,4]{1,3,2,0:T(4,128)S(1)}, u32[]{:S(2)}, u32[]{:S(2)}) %all-to-all-start.9) | async-done | bytes 6176 | tf_op jit(solution)/shard_map/all_to_all | solution.py:42
  328.7 4.8 collective-permute-start.18
  334.9 3.2 collective-permute-done.19
  339.1 5.9 %all-to-all-start.10 = ((f32[64,6,1,4]{1,3,2,0:T(4,128)}), f32[64,6,1,4]{1,3,2,0:T(4,128)S(1)}, u32[]{:S(2)}, u32[]{:S(2)}) async-start(f32[64,6,1,4]{1,3,2,0:T(4,128)} %broadcast_in_dim.320), calls=%async_computation.10 | async-start | bytes 262144 | tf_op jit(solution)/shard_map/all_to_all | solution.py:42
  345.0 11.2 %all-to-all-done.10 = f32[64,6,1,4]{1,3,2,0:T(4,128)S(1)} async-done(((f32[64,6,1,4]{1,3,2,0:T(4,128)}), f32[64,6,1,4]{1,3,2,0:T(4,128)S(1)}, u32[]{:S(2)}, u32[]{:S(2)}) %all-to-all-start.10) | async-done | bytes 6176 | tf_op jit(solution)/shard_map/all_to_all | solution.py:42
  358.8 3.6 collective-permute-start.20
  363.8 3.0 collective-permute-done.21
  367.9 5.9 %all-to-all-start.11 = ((f32[64,6,1,16]{3,2,1,0:T(1,128)}), f32[64,6,1,16]{3,2,1,0:T(1,128)S(1)}, u32[]{:S(2)}, u32[]{:S(2)}) async-start(f32[64,6,1,16]{3,2,1,0:T(1,128)} %broadcast_in_dim.327), calls=%async_computation.11 | async-start | bytes 393216 | tf_op jit(solution)/shard_map/all_to_all | solution.py:42
  373.7 12.2 %all-to-all-done.11 = f32[64,6,1,16]{3,2,1,0:T(1,128)S(1)} async-done(((f32[64,6,1,16]{3,2,1,0:T(1,128)}), f32[64,6,1,16]{3,2,1,0:T(1,128)S(1)}, u32[]{:S(2)}, u32[]{:S(2)}) %all-to-all-start.11) | async-done | bytes 24608 | tf_op jit(solution)/shard_map/all_to_all | solution.py:42
  388.8 2.9 collective-permute-start.22
  393.0 3.0 collective-permute-done.23
  398.3 5.9 %all-to-all-start.12 = ((f32[64,1,384]{2,1,0:T(1,128)}), f32[64,1,384]{2,1,0:T(1,128)S(1)}, u32[]{:S(2)}, u32[]{:S(2)}) async-start(f32[64,1,384]{2,1,0:T(1,128)} %reshape.2447), calls=%async_computation.12 | async-start | bytes 196608 | tf_op jit(solution)/shard_map/all_to_all | solution.py:42
  404.2 10.7 %all-to-all-done.12 = f32[64,1,384]{2,1,0:T(1,128)S(1)} async-done(((f32[64,1,384]{2,1,0:T(1,128)}), f32[64,1,384]{2,1,0:T(1,128)S(1)}, u32[]{:S(2)}, u32[]{:S(2)}) %all-to-all-start.12) | async-done | bytes 98336 | tf_op jit(solution)/shard_map/all_to_all | solution.py:42
  419.3 2.9 collective-permute-start.24
  423.5 3.0 collective-permute-done.25
  427.7 6.4 %all-to-all-start.13 = ((f32[64,6,1,256]{3,2,1,0:T(1,128)}), f32[64,6,1,256]{3,2,1,0:T(1,128)S(1)}, u32[]{:S(2)}, u32[]{:S(2)}) async-start(f32[64,6,1,256]{3,2,1,0:T(1,128)} %broadcast_in_dim.337), calls=%async_computation.13 | async-start | bytes 786432 | tf_op jit(solution)/shard_map/all_to_all | solution.py:42
  434.2 15.2 %all-to-all-done.13 = f32[64,6,1,256]{3,2,1,0:T(1,128)S(1)} async-done(((f32[64,6,1,256]{3,2,1,0:T(1,128)}), f32[64,6,1,256]{3,2,1,0:T(1,128)S(1)}, u32[]{:S(2)}, u32[]{:S(2)}) %all-to-all-start.13) | async-done | bytes 393248 | tf_op jit(solution)/shard_map/all_to_all | solution.py:42
  454.9 2.9 collective-permute-start.26
  459.1 3.0 collective-permute-done.27
  463.0 5.0 all_to_all.118
  469.2 13.2 %all_to_all.119 = f32[32,1,192]{2,1,0:T(1,128)S(1)} all-to-all(f32[32,1,192]{2,1,0:T(1,128)S(1)} %reshape.2451), channel_id=1, replica_groups=mesh['gx'=8,'gy_0'=8,'gy_1'=4,'gy_2'=2] {'gy_0','gy_1'}, dimensions={0} | all-to-all | bytes 49152 | tf_op jit(solution)/shard_map/all_to_all | solution.py:30
  488.2 15.1 %all_to_all.120 = f32[2,64,16]{2,0,1:T(2,128)S(1)} all-to-all(f32[2,64,16]{2,0,1:T(2,128)S(1)} %copy.679), channel_id=1, replica_groups=mesh['gx'=8,'gy_0'=8,'gy_1'=4,'gy_2'=2] {'gy_0','gy_1','gy_2'}, dimensions={1} | all-to-all | bytes 16384 | tf_op jit(solution)/shard_map/all_to_all | solution.py:244
  505.6 2.9 collective-permute-start.28
  509.9 2.9 collective-permute-done.29
  513.5 5.3 all_to_all.121
  520.8 4.0 all-to-all-start.18
  524.9 9.0 %all-to-all-done.18 = f32[32,1,768]{2,1,0:T(1,128)S(1)} async-done(((f32[32,1,768]{2,1,0:T(1,128)}), f32[32,1,768]{2,1,0:T(1,128)S(1)}, u32[]{:S(2)}, u32[]{:S(2)}) %all-to-all-start.18) | async-done | bytes 98336 | tf_op jit(solution)/shard_map/all_to_all | solution.py:30
  540.5 5.7 %all-to-all-start.19 = ((f32[64,1,128]{2,1,0:T(1,128)}), f32[64,1,128]{2,1,0:T(1,128)S(1)}, u32[]{:S(2)}, u32[]{:S(2)}) async-start(f32[64,1,128]{2,1,0:T(1,128)} %reshape.2457), calls=%async_computation.19 | async-start | bytes 65536 | tf_op jit(solution)/shard_map/all_to_all | solution.py:244
  546.3 9.5 %all-to-all-done.19 = f32[64,1,128]{2,1,0:T(1,128)S(1)} async-done(((f32[64,1,128]{2,1,0:T(1,128)}), f32[64,1,128]{2,1,0:T(1,128)S(1)}, u32[]{:S(2)}, u32[]{:S(2)}) %all-to-all-start.19) | async-done | bytes 32800 | tf_op jit(solution)/shard_map/all_to_all | solution.py:244
  (3020 shorter events, 150.8 us)
Async XLA Ops:
  2.1 24.5 %collective-permute-start.3 = (f32[3,1,32,128]{3,2,1,0:T(8,128)S(1)}, f32[3,1,32,128]{3,2,1,0:T(8,128)S(1)}, u32[]{:S(2)}, u32[]{:S(2)}) collective-permute-start(f32[3,1,32,128]{3,2,1,0:T(8,128)S(1)} %get-tuple-element.611), channel_id=1, source_target_pairs={{0,1},{1,2},{2,3},{3,4},{4,5},{5,6},{6,7},{7,8},{8,9},{9,10},{10,1... | collective-permute-start | bytes 147464 | tf_op jit(solution)/shard_map/ppermute | solution.py:75
  5.8 20.8 %collective-permute-start = (f32[3,8,1,128]{3,2,1,0:T(1,128)S(1)}, f32[3,8,1,128]{3,2,1,0:T(1,128)S(1)}, u32[]{:S(2)}, u32[]{:S(2)}) collective-permute-start(f32[3,8,1,128]{3,2,1,0:T(1,128)S(1)} %get-tuple-element.613), channel_id=1, source_target_pairs={{64,0},{128,64},{192,128},{256,192},{320,256},{384,320},{448,384},... | collective-permute-start | bytes 36872 | tf_op jit(solution)/shard_map/ppermute | solution.py:76
  8.8 17.8 %collective-permute-start.1 = (f32[3,8,1,128]{3,2,1,0:T(1,128)S(1)}, f32[3,8,1,128]{3,2,1,0:T(1,128)S(1)}, u32[]{:S(2)}, u32[]{:S(2)}) collective-permute-start(f32[3,8,1,128]{3,2,1,0:T(1,128)S(1)} %get-tuple-element.612), channel_id=1, source_target_pairs={{0,64},{64,128},{128,192},{192,256},{256,320},{320,384},{384,448},... | collective-permute-start | bytes 36872 | tf_op jit(solution)/shard_map/ppermute | solution.py:75
  10.1 16.6 %collective-permute-start.2 = (f32[3,1,32,128]{3,2,1,0:T(8,128)S(1)}, f32[3,1,32,128]{3,2,1,0:T(8,128)S(1)}, u32[]{:S(2)}, u32[]{:S(2)}) collective-permute-start(f32[3,1,32,128]{3,2,1,0:T(8,128)S(1)} %get-tuple-element.610), channel_id=1, source_target_pairs={{1,0},{2,1},{3,2},{4,3},{5,4},{6,5},{7,6},{8,7},{9,8},{10,9},{11,1... | collective-permute-start | bytes 147464 | tf_op jit(solution)/shard_map/ppermute | solution.py:76
  38.2 39.8 %all-to-all-start.1 = ((f32[32,1,768]{2,1,0:T(1,128)}), f32[32,1,768]{2,1,0:T(1,128)}, u32[]{:S(2)}, u32[]{:S(2)}) async-start(f32[32,1,768]{2,1,0:T(1,128)} %reshape.2437), calls=%async_computation.1 | async-start | bytes 196608 | tf_op jit(solution)/shard_map/all_to_all | solution.py:30
  71.1 112.2 %copy-start.3 = (f32[4,16,64]{2,1,0:T(8,128)}, f32[4,16,64]{2,1,0:T(8,128)S(1)}, u32[]{:S(2)}) copy-start(f32[4,16,64]{2,1,0:T(8,128)S(1)} %get-tuple-element.1484) | copy-start | bytes 49156
  72.5 103.2 %copy-start.33 = (f32[4,16,64]{2,1,0:T(8,128)}, f32[4,16,64]{2,1,0:T(8,128)S(1)}, u32[]{:S(2)}) copy-start(f32[4,16,64]{2,1,0:T(8,128)S(1)} %get-tuple-element.864) | copy-start | bytes 49156
  72.5 103.3 %copy-start.32 = (f32[4,16,64]{2,1,0:T(8,128)}, f32[4,16,64]{2,1,0:T(8,128)S(1)}, u32[]{:S(2)}) copy-start(f32[4,16,64]{2,1,0:T(8,128)S(1)} %get-tuple-element.867) | copy-start | bytes 49156
  72.7 103.2 %copy-start.28 = (f32[1,16,64]{2,1,0:T(8,128)}, f32[1,16,64]{2,1,0:T(8,128)S(1)}, u32[]{:S(2)}) copy-start(f32[1,16,64]{2,1,0:T(8,128)S(1)} %get-tuple-element.497) | copy-start | bytes 12292
  85.5 20.1 %all-to-all-start.2 = ((f32[64,1,128]{2,1,0:T(1,128)}), f32[64,1,128]{2,1,0:T(1,128)S(1)}, u32[]{:S(2)}, u32[]{:S(2)}) async-start(f32[64,1,128]{2,1,0:T(1,128)} %reshape.2439), calls=%async_computation.2 | async-start | bytes 65536 | tf_op jit(solution)/shard_map/all_to_all | solution.py:244
  107.8 5.4 collective-permute-start.4
  111.8 4.4 collective-permute-start.5
  140.5 13.0 %all-to-all-start.4 = ((f32[32,1,192]{2,1,0:T(1,128)}), f32[32,1,192]{2,1,0:T(1,128)S(1)}, u32[]{:S(2)}, u32[]{:S(2)}) async-start(f32[32,1,192]{2,1,0:T(1,128)} %reshape.2443), calls=%async_computation.4 | async-start | bytes 65536 | tf_op jit(solution)/shard_map/all_to_all | solution.py:30
  159.9 15.6 %all-to-all-start.5 = ((f32[2,64,16]{2,0,1:T(2,128)}), f32[2,64,16]{2,0,1:T(2,128)S(1)}, u32[]{:S(2)}, u32[]{:S(2)}) async-start(f32[2,64,16]{2,0,1:T(2,128)} %copy.577), calls=%async_computation.5 | async-start | bytes 131072 | tf_op jit(solution)/shard_map/all_to_all | solution.py:244
  176.0 4.4 collective-permute-start.6
  179.0 4.3 collective-permute-start.7
  186.8 4.6 collective-permute-start.8
  193.1 19.8 %all-to-all-start.6 = ((f32[64,6,1,256]{3,2,1,0:T(1,128)}), f32[64,6,1,256]{3,2,1,0:T(1,128)S(1)}, u32[]{:S(2)}, u32[]{:S(2)}) async-start(f32[64,6,1,256]{3,2,1,0:T(1,128)} %broadcast_in_dim.282), calls=%async_computation.6 | async-start | bytes 786432 | tf_op jit(solution)/shard_map/all_to_all | solution.py:42
  218.0 6.0 %collective-permute-start.10 = (f32[4,1,32]{2,1,0:T(1,128)S(1)}, f32[4,1,32]{2,1,0:T(1,128)S(1)}, u32[]{:S(2)}, u32[]{:S(2)}) collective-permute-start(f32[4,1,32]{2,1,0:T(1,128)S(1)} %get-tuple-element.969), channel_id=1, source_target_pairs={{0,64},{64,128},{128,192},{192,256},{256,320},{320,384},{384,448},... | collective-permute-start | bytes 1544 | tf_op jit(solution)/shard_map/ppermute | solution.py:58
  219.4 5.2 collective-permute-start.9
  225.1 4.6 collective-permute-start.11
  232.6 18.0 %all-to-all-start.7 = ((f32[64,1,384]{2,1,0:T(1,128)}), f32[64,1,384]{2,1,0:T(1,128)S(1)}, u32[]{:S(2)}, u32[]{:S(2)}) async-start(f32[64,1,384]{2,1,0:T(1,128)} %reshape.2445), calls=%async_computation.7 | async-start | bytes 196608 | tf_op jit(solution)/shard_map/all_to_all | solution.py:42
  254.8 5.3 collective-permute-start.12
  258.7 4.6 collective-permute-start.13
  263.7 6.0 %collective-permute-start.14 = (f32[7,2,2,8]{3,2,1,0:T(2,128)S(1)}, f32[7,2,2,8]{3,2,1,0:T(2,128)S(1)}, u32[]{:S(2)}, u32[]{:S(2)}) collective-permute-start(f32[7,2,2,8]{3,2,1,0:T(2,128)S(1)} %constant_dynamic-update-slice_fusion.62), channel_id=1, source_target_pairs={{0,4},{1,5},{2,6},{3,7},{4,0},{5,1},{6,2},{7,3},{8,12},{9,13},{10,... | collective-permute-start | bytes 2696 | tf_op jit(solution)/shard_map/ppermute | solution.py:88
  271.3 19.0 %all-to-all-start.8 = ((f32[64,6,1,16]{3,2,1,0:T(1,128)}), f32[64,6,1,16]{3,2,1,0:T(1,128)S(1)}, u32[]{:S(2)}, u32[]{:S(2)}) async-start(f32[64,6,1,16]{3,2,1,0:T(1,128)} %broadcast_in_dim.306), calls=%async_computation.8 | async-start | bytes 393216 | tf_op jit(solution)/shard_map/all_to_all | solution.py:42
  292.6 5.2 collective-permute-start.15
  296.4 6.1 %collective-permute-start.16 = (f32[4,1,8]{2,1,0:T(1,128)S(1)}, f32[4,1,8]{2,1,0:T(1,128)S(1)}, u32[]{:S(2)}, u32[]{:S(2)}) collective-permute-start(f32[4,1,8]{2,1,0:T(1,128)S(1)} %get-tuple-element.1214), channel_id=1, source_target_pairs={{0,64},{64,128},{128,192},{192,256},{256,320},{320,384},{384,448},... | collective-permute-start | bytes 392 | tf_op jit(solution)/shard_map/ppermute | solution.py:58
  302.9 4.4 collective-permute-start.17
  308.2 18.1 %all-to-all-start.9 = ((f32[64,6,1,4]{1,3,2,0:T(4,128)}), f32[64,6,1,4]{1,3,2,0:T(4,128)S(1)}, u32[]{:S(2)}, u32[]{:S(2)}) async-start(f32[64,6,1,4]{1,3,2,0:T(4,128)} %broadcast_in_dim.318), calls=%async_computation.9 | async-start | bytes 262144 | tf_op jit(solution)/shard_map/all_to_all | solution.py:42
  328.7 6.2 %collective-permute-start.18 = (f32[4,1,4]{2,0,1:T(4,128)S(1)}, f32[4,1,4]{2,0,1:T(4,128)S(1)}, u32[]{:S(2)}, u32[]{:S(2)}) collective-permute-start(f32[4,1,4]{2,0,1:T(4,128)S(1)} %fusion.222), channel_id=1, source_target_pairs={{64,0},{128,64},{192,128},{256,192},{320,256},{384,320},{448,384},... | collective-permute-start | bytes 200 | tf_op jit(solution)/shard_map/ppermute | solution.py:60
  333.5 4.6 collective-permute-start.19
  339.1 17.1 %all-to-all-start.10 = ((f32[64,6,1,4]{1,3,2,0:T(4,128)}), f32[64,6,1,4]{1,3,2,0:T(4,128)S(1)}, u32[]{:S(2)}, u32[]{:S(2)}) async-start(f32[64,6,1,4]{1,3,2,0:T(4,128)} %broadcast_in_dim.320), calls=%async_computation.10 | async-start | bytes 262144 | tf_op jit(solution)/shard_map/all_to_all | solution.py:42
  358.8 5.0 collective-permute-start.20
  362.4 4.3 collective-permute-start.21
  367.9 18.1 %all-to-all-start.11 = ((f32[64,6,1,16]{3,2,1,0:T(1,128)}), f32[64,6,1,16]{3,2,1,0:T(1,128)S(1)}, u32[]{:S(2)}, u32[]{:S(2)}) async-start(f32[64,6,1,16]{3,2,1,0:T(1,128)} %broadcast_in_dim.327), calls=%async_computation.11 | async-start | bytes 393216 | tf_op jit(solution)/shard_map/all_to_all | solution.py:42
  386.0 68.8 %copy-start.29 = (f32[1,16,64]{2,1,0:T(8,128)S(1)}, f32[1,16,64]{2,1,0:T(8,128)}, u32[]{:S(2)}) copy-start(f32[1,16,64]{2,1,0:T(8,128)} %copy-done.28) | copy-start | bytes 12292
  386.0 68.7 %copy-start.46 = (f32[1,16,64]{2,1,0:T(8,128)S(1)}, f32[1,16,64]{2,1,0:T(8,128)}, u32[]{:S(2)}) copy-start(f32[1,16,64]{2,1,0:T(8,128)} %copy-done.45) | copy-start | bytes 12292
  386.0 68.7 %copy-start.48 = (f32[1,16,64]{2,1,0:T(8,128)S(1)}, f32[1,16,64]{2,1,0:T(8,128)}, u32[]{:S(2)}) copy-start(f32[1,16,64]{2,1,0:T(8,128)} %copy-done.47) | copy-start | bytes 12292
  386.0 68.7 %copy-start.53 = (f32[1,16,64]{2,1,0:T(8,128)S(1)}, f32[1,16,64]{2,1,0:T(8,128)}, u32[]{:S(2)}) copy-start(f32[1,16,64]{2,1,0:T(8,128)} %copy-done.52) | copy-start | bytes 12292
  386.0 68.7 %copy-start.55 = (f32[1,16,64]{2,1,0:T(8,128)S(1)}, f32[1,16,64]{2,1,0:T(8,128)}, u32[]{:S(2)}) copy-start(f32[1,16,64]{2,1,0:T(8,128)} %copy-done.54) | copy-start | bytes 12292
  387.0 75.1 %copy-start.4 = (f32[4,16,64]{2,1,0:T(8,128)S(1)}, f32[4,16,64]{2,1,0:T(8,128)}, u32[]{:S(2)}) copy-start(f32[4,16,64]{2,1,0:T(8,128)} %copy-done.3) | copy-start | bytes 49156
  387.0 75.1 %copy-start.16 = (f32[4,16,64]{2,1,0:T(8,128)S(1)}, f32[4,16,64]{2,1,0:T(8,128)}, u32[]{:S(2)}) copy-start(f32[4,16,64]{2,1,0:T(8,128)} %copy-done.15) | copy-start | bytes 49156
  387.6 74.6 %copy-start.6 = (f32[4,16,64]{2,1,0:T(8,128)S(1)}, f32[4,16,64]{2,1,0:T(8,128)}, u32[]{:S(2)}) copy-start(f32[4,16,64]{2,1,0:T(8,128)} %copy-done.5) | copy-start | bytes 49156
  387.6 74.6 %copy-start.14 = (f32[4,16,64]{2,1,0:T(8,128)S(1)}, f32[4,16,64]{2,1,0:T(8,128)}, u32[]{:S(2)}) copy-start(f32[4,16,64]{2,1,0:T(8,128)} %copy-done.13) | copy-start | bytes 49156
  387.6 74.6 %copy-start.51 = (f32[1,16,64]{2,1,0:T(8,128)S(1)}, f32[1,16,64]{2,1,0:T(8,128)}, u32[]{:S(2)}) copy-start(f32[1,16,64]{2,1,0:T(8,128)} %copy-done.50) | copy-start | bytes 12292
  387.6 74.6 %copy-start.69 = (f32[1,16,64]{2,1,0:T(8,128)S(1)}, f32[1,16,64]{2,1,0:T(8,128)}, u32[]{:S(2)}) copy-start(f32[1,16,64]{2,1,0:T(8,128)} %copy-done.68) | copy-start | bytes 12292
  388.0 74.3 %copy-start.38 = (f32[1,16,64]{2,1,0:T(8,128)S(1)}, f32[1,16,64]{2,1,0:T(8,128)}, u32[]{:S(2)}) copy-start(f32[1,16,64]{2,1,0:T(8,128)} %copy-done.37) | copy-start | bytes 12292
  388.0 74.3 %copy-start.40 = (f32[1,16,64]{2,1,0:T(8,128)S(1)}, f32[1,16,64]{2,1,0:T(8,128)}, u32[]{:S(2)}) copy-start(f32[1,16,64]{2,1,0:T(8,128)} %copy-done.39) | copy-start | bytes 12292
  388.0 74.3 %copy-start.42 = (f32[1,16,64]{2,1,0:T(8,128)S(1)}, f32[1,16,64]{2,1,0:T(8,128)}, u32[]{:S(2)}) copy-start(f32[1,16,64]{2,1,0:T(8,128)} %copy-done.41) | copy-start | bytes 12292
  388.0 74.3 %copy-start.44 = (f32[1,16,64]{2,1,0:T(8,128)S(1)}, f32[1,16,64]{2,1,0:T(8,128)}, u32[]{:S(2)}) copy-start(f32[1,16,64]{2,1,0:T(8,128)} %copy-done.43) | copy-start | bytes 12292
  388.7 73.8 %copy-start.34 = (f32[6,1,64,16]{2,3,1,0:T(8,128)S(1)}, f32[6,1,64,16]{2,3,1,0:T(8,128)}, u32[]{:S(2)}) copy-start(f32[6,1,64,16]{2,3,1,0:T(8,128)} %copy.920) | copy-start | bytes 73732
  388.8 4.2 collective-permute-start.22
  391.6 4.3 collective-permute-start.23
  398.3 16.6 %all-to-all-start.12 = ((f32[64,1,384]{2,1,0:T(1,128)}), f32[64,1,384]{2,1,0:T(1,128)S(1)}, u32[]{:S(2)}, u32[]{:S(2)}) async-start(f32[64,1,384]{2,1,0:T(1,128)} %reshape.2447), calls=%async_computation.12 | async-start | bytes 196608 | tf_op jit(solution)/shard_map/all_to_all | solution.py:42
  419.3 4.2 collective-permute-start.24
  422.1 4.3 collective-permute-start.25
  427.7 21.6 %all-to-all-start.13 = ((f32[64,6,1,256]{3,2,1,0:T(1,128)}), f32[64,6,1,256]{3,2,1,0:T(1,128)S(1)}, u32[]{:S(2)}, u32[]{:S(2)}) async-start(f32[64,6,1,256]{3,2,1,0:T(1,128)} %broadcast_in_dim.337), calls=%async_computation.13 | async-start | bytes 786432 | tf_op jit(solution)/shard_map/all_to_all | solution.py:42
  454.9 4.2 collective-permute-start.26
  457.8 4.3 collective-permute-start.27
  505.6 4.3 collective-permute-start.28
  508.4 4.4 collective-permute-start.29
  520.8 13.1 %all-to-all-start.18 = ((f32[32,1,768]{2,1,0:T(1,128)}), f32[32,1,768]{2,1,0:T(1,128)S(1)}, u32[]{:S(2)}, u32[]{:S(2)}) async-start(f32[32,1,768]{2,1,0:T(1,128)} %reshape.2455), calls=%async_computation.18 | async-start | bytes 196608 | tf_op jit(solution)/shard_map/all_to_all | solution.py:30
  540.5 15.3 %all-to-all-start.19 = ((f32[64,1,128]{2,1,0:T(1,128)}), f32[64,1,128]{2,1,0:T(1,128)S(1)}, u32[]{:S(2)}, u32[]{:S(2)}) async-start(f32[64,1,128]{2,1,0:T(1,128)} %reshape.2457), calls=%async_computation.19 | async-start | bytes 65536 | tf_op jit(solution)/shard_map/all_to_all | solution.py:244
  (55 other events, 2452.9 us)
where the time goes:
time: 566 us; the launch traced here: 559 us
  waiting for transfers between devices  178 us (31%)
  starting transfers between devices  170 us (30%)
  local copies, waits for them, and re-layouts  103 us (18%)
  other arithmetic  50.7 us (9%)
  blocking collectives  47.6 us (8%)
  between operations  10 us (2%)
    all_to_all x8, waiting for transfers between devices, copy_for_each(): lax.all_to_all(jnp.broadcast_to(x[None], (count, *x.shape)), axis, 0, 0,...  94.7 us
    all_to_all x8, starting transfers between devices, copy_for_each(): lax.all_to_all(jnp.broadcast_to(x[None], (count, *x.shape)), axis, 0, 0,...  49.3 us
    ppermute x11, starting transfers between devices, padded(): lax.ppermute(head, axis, [((i + 1) % count, i) for i in range(ends)])  39 us
    all_to_all x5, blocking collectives, turned_blocks(): lax.all_to_all(parts, axes[k], split_axis=k, concat_axis=k, tiled=True)  32.5 us
    ppermute x11, waiting for transfers between devices, padded(): lax.ppermute(tail, axis, [(i, (i + 1) % count) for i in range(ends)])  31.8 us
    all_to_all x3, waiting for transfers between devices, reduced_moved(): lax.all_to_all(jnp.stack([prev_last, next_first]), GY, split_axis=1, conc...  26.4 us
    all_to_all x3, starting transfers between devices, turned_blocks(): lax.all_to_all(parts, axes[k], split_axis=k, concat_axis=k, tiled=True)  23.1 us
    all_to_all x3, starting transfers between devices, reduced_moved(): lax.all_to_all(jnp.stack([prev_last, next_first]), GY, split_axis=1, conc...  21.9 us
  transfers between devices with their start and end apart: 44, of which 28 were waited for; matrix products, arithmetic and copies ran while one was open for 8% of the time, Pallas kernels for 0%

commit v1 on v0

--- a/solution.py
+++ b/solution.py
@@ -278,6 +278,60 @@
     return line_solve(level, rhs + neighbour_terms(level, field))
 
 
+WHOLE_FROM = 3
+
+
+def gather_whole(block, depth):
+    if depth == 2:
+        axes, count = (("gx",) + GY, lax.axis_size(GY))
+    else:
+        axes, count = (("gx", "gy_0", "gy_1"), lax.axis_size(GY) // 2)
+    parts = lax.all_gather(block, axes, axis=0)
+    parts = parts.reshape(lax.axis_size("gx"), count, *block.shape)
+    parts = jnp.moveaxis(parts, (0, 1), (3, 1))
+    lead, rows, width, height = (block.shape[0], block.shape[1], block.shape[2], block.shape[3])
+    return parts.reshape(lead, count * rows, lax.axis_size("gx") * width, height)
+
+
+def whole_level(face_x, face_y, face_z, shift):
+    low_x = behind(face_x, 1)
+    low_y = behind(face_y, 0)
+    low_z = behind(face_z, 2)
+    diag = shift + face_x + low_x + face_y + low_y + face_z + low_z
+    level = {
+        "face_x": face_x,
+        "low_x": low_x,
+        "face_y": face_y,
+        "low_y": low_y,
+        "face_z": face_z,
+        "low_z": low_z,
+        "diag": diag,
+        "lower": -low_y,
+    }
+    level["denoms"], level["ratios"] = line_factors(-low_y, diag, -face_y)
+    return level
+
+
+def whole_terms(level, field):
+    return (
+        level["face_x"] * ahead(field, 1)
+        + level["low_x"] * behind(field, 1)
+        + level["face_z"] * ahead(field, 2)
+        + level["low_z"] * behind(field, 2)
+    )
+
+
+def whole_cycle(levels, depth, rhs):
+    level = levels[depth]
+    field = rows_solve(level, rhs)
+    if depth == len(levels) - 1:
+        return rows_solve(level, rhs + whole_terms(level, field))
+    residual = whole_terms(level, field)
+    correction = whole_cycle(levels, depth + 1, 0.25 * coarse_sum(residual))
+    field = field + prolong(correction)
+    return rows_solve(level, rhs + whole_terms(level, field))
+
+
 def body(source, mask, cond_x, cond_y, cond_z):
     open_cells = (mask != 2).astype(jnp.float32)
     wall = (mask == 1).astype(jnp.float32)
@@ -297,7 +351,7 @@
     fields = []
     sources = []
     residual = rhs
-    for depth in range(LEVELS):
+    for depth in range(WHOLE_FROM):
         group = 1
         if depth > 0:
             face_x, low_x, face_y, low_y, face_z, shift = faces
@@ -322,16 +376,39 @@
                 faces = tuple((folded[place] for place in range(1, 7)))
         level = assemble(faces, group)
         field = line_solve(level, rhs)
-        if depth == LEVELS - 1:
-            field = relax(level, field, rhs)
-        else:
-            residual = neighbour_terms(level, field)
+        residual = neighbour_terms(level, field)
         levels.append(level)
         fields.append(field)
         sources.append(rhs)
-    correction = fields[-1]
-    for depth in range(LEVELS - 2, -1, -1):
-        if depth + 1 >= 2:
+    face_x, low_x, face_y, low_y, face_z, shift = faces
+    coarse = jnp.stack(
+        [
+            coarse_face(face_x, 1, 1),
+            coarse_face(face_y, 0, 1),
+            coarse_face(face_z, 2, 1),
+            0.25 * coarse_sum(shift),
+        ]
+    )
+    whole = gather_whole(coarse, WHOLE_FROM)
+    whole_rhs = gather_whole((0.25 * coarse_sum(residual))[None], WHOLE_FROM)[0]
+    face_x, face_y, face_z, shift = (whole[0], whole[1], whole[2], whole[3])
+    chain = [whole_level(face_x, face_y, face_z, shift)]
+    for depth in range(WHOLE_FROM + 1, LEVELS):
+        face_x = coarse_face(face_x, 1, 1)
+        face_y = coarse_face(face_y, 0, 1)
+        face_z = coarse_face(face_z, 2, 1)
+        shift = 0.25 * coarse_sum(shift)
+        chain.append(whole_level(face_x, face_y, face_z, shift))
+    whole_correction = whole_cycle(chain, 0, whole_rhs)
+    rows, width, height = coarse.shape[1:]
+    spread = 2 ** max(WHOLE_FROM - 2, 0)
+    correction = lax.dynamic_slice(
+        whole_correction,
+        (rows * (lax.axis_index(GY) // spread), width * lax.axis_index("gx"), 0),
+        (rows, width, height),
+    )
+    for depth in range(WHOLE_FROM - 1, -1, -1):
+        if depth < WHOLE_FROM - 1 and depth + 1 >= 2:
             half = correction.shape[0] // 2
             correction = lax.dynamic_slice_in_dim(correction, upper_flag(depth - 1) * half, half, 0)
         field = fields[depth] + prolong(correction)

time: 566 us -> 2370 us (4.19)
  blocking collectives: 47.6 us -> 1070 us
  local copies, waits for them, and re-layouts: 103 us -> 494 us
  starting transfers between devices: 170 us -> 464 us
  other arithmetic: 50.7 us -> 229 us
  waiting for transfers between devices: 178 us -> 78.1 us
    all_gather x0 -> x2, blocking collectives: none -> 1020 us  [gather_whole(): parts = lax.all_gather(block, axes, axis=0)]
    all_to_all x8 -> x2, starting transfers between devices: 49.3 us -> 372 us  [copy_for_each(): lax.all_to_all(jnp.broadcast_to(x[None], (count, *x.shape)), axis, 0, 0,...]
    slice x940 -> x706, local copies, waits for them, and re-layouts: 16.3 us -> 139 us  [reduced_local(): inclusive = lax.associative_scan(chain_forward, terms, axis=0)]
    all_to_all x8 -> x2, waiting for transfers between devices: 94.7 us -> 14.5 us  [copy_for_each(): lax.all_to_all(jnp.broadcast_to(x[None], (count, *x.shape)), axis, 0, 0,...]
    sub x0 -> x42, local copies, waits for them, and re-layouts: none -> 42 us  [rows_solve(): result.append(values[place] - ratios[place] * result[-1])]
    slice x312 -> x214, local copies, waits for them, and re-layouts: 5.85 us -> 43.6 us  [reduced_local(): lax.associative_scan(chain_backward, (start, slope), reverse=True, axis=0)]
    another operation x4 -> x33, local copies, waits for them, and re-layouts: 2.54 us -> 40.2 us  [rows_solve(): return jnp.stack(result[::-1])]
    pad x192 -> x132, local copies, waits for them, and re-layouts: 1.98 us -> 34.8 us  [reduced_local(): inclusive = lax.associative_scan(chain_forward, terms, axis=0)]
  transfers between devices with their start and end apart: 44 -> 25, of which waited for: 28 -> 13; matrix products, arithmetic and copies ran while one was open for 8% -> 4% of each run, Pallas kernels for 0% -> 0%
where the time goes in v1:
time: 2370 us; the launch traced here: 2340 us
  blocking collectives  1070 us (45%)
  local copies, waits for them, and re-layouts  494 us (21%)
  starting transfers between devices  464 us (20%)
  other arithmetic  229 us (10%)
  waiting for transfers between devices  78.1 us (3%)
    all_gather x2, blocking collectives, gather_whole(): parts = lax.all_gather(block, axes, axis=0)  1020 us
    all_to_all x2, starting transfers between devices, copy_for_each(): lax.all_to_all(jnp.broadcast_to(x[None], (count, *x.shape)), axis, 0, 0,...  372 us
    slice x706, local copies, waits for them, and re-layouts, reduced_local(): inclusive = lax.associative_scan(chain_forward, terms, axis=0)  139 us
  transfers between devices with their start and end apart: 25, of which 13 were waited for; matrix products, arithmetic and copies ran while one was open for 4% of the time, Pallas kernels for 0%

profile of v1, /device:TPU:57, one launch (start us, length us, event | category | flops | bytes accessed | tf_op | source)
XLA Modules:
  0.0 2341.1 jit_solution(15719183095452096029)
XLA Ops:
  2.1 3.7 collective-permute-start.3
  7.1 4.0 collective-permute-start
  13.1 9.7 reshape.649
  22.9 4.7 reduce_sum.270
  29.2 2.4 slice.7159
  33.6 3.5 all_to_all.86
  39.6 14.6 all-to-all-start.1
  72.9 10.7 all-to-all-start.2
  83.7 9.4 all-to-all-done.2
  95.1 3.0 collective-permute-start.4
  99.5 2.9 collective-permute-done.5
  102.6 9.7 reshape.648
  112.3 4.0 reduce_sum.268
  118.2 5.5 all_to_all.87
  125.5 4.0 all-to-all-start.4
  130.4 7.9 all-to-all-done.4
  144.6 5.4 all-to-all-start.5
  151.3 8.8 all-to-all-done.5
  160.6 3.5 collective-permute-start.6
  165.5 3.2 collective-permute-done.7
  170.2 3.5 collective-permute-start.8
  176.4 514.1 %all-gather.1 = f32[1024,2,4,16]{3,2,1,0:T(4,128)S(1)} all-gather(f32[4,2,4,16]{3,2,1,0:T(4,128)S(1)} %pad_maximum_fusion.47), channel_id=3, replica_groups=mesh['gx'=8,'gy_0'=8,'gy_1'=4,'gy_2'=2] {'gx','gy_0','gy_1'}, dimensions={0}, use_global_device_ids=true | all-gather | bytes 526336 | tf_op jit(solution)/shard_map/all_gather | solution.py:289
  691.8 3.0 slice_reduce_fusion.8
  716.5 187.0 %all-to-all-start.6 = ((f32[64,6,1,256]{3,2,1,0:T(1,128)}), f32[64,6,1,256]{3,2,1,0:T(1,128)}, u32[]{:S(2)}, u32[]{:S(2)}) async-start(f32[64,6,1,256]{3,2,1,0:T(1,128)} %broadcast_in_dim.193), calls=%async_computation.6 | async-start | bytes 786432 | tf_op jit(solution)/shard_map/all_to_all | solution.py:42
  903.4 2.1 copy.1201
  913.3 2.1 slice.7908
  915.4 2.1 copy.1198
  917.5 2.1 copy.1199
  932.1 5.1 slice.7913
  937.2 2.3 copy.1206
  945.7 2.1 broadcast_multiply_fusion.3
  956.0 2.5 mul.28970
  964.7 3.7 add_add_fusion.1
  1296.1 3.0 collective-permute-done.10
  1304.6 503.7 %all-gather = f32[512,4,16]{2,1,0:T(4,128)S(1)} all-gather(f32[2,4,16]{2,1,0:T(4,128)S(1)} %broadcast_multiply_fusion.16), channel_id=2, replica_groups=mesh['gx'=8,'gy_0'=8,'gy_1'=4,'gy_2'=2] {'gx','gy_0','gy_1'}, dimensions={0}, use_global_device_ids=true | all-gather | bytes 131584 | tf_op jit(solution)/shard_map/all_gather | solution.py:289
  1808.6 2.0 subtract_divide_fusion.73
  1817.6 2.3 constant_dynamic-update-slice_fusion.111
  1835.1 2.1 multiply_add_fusion
  1837.1 2.5 copy.1196
  1839.6 11.0 reshape.658
  1850.6 4.7 reduce_sum.287
  1858.6 2.3 constant_dynamic-update-slice_fusion.144
  1865.9 2.4 reshape.659
  1895.4 2.7 copy.1224
  1904.1 2.5 multiply_subtract_fusion.25
  1948.7 2.5 fusion.469
  1980.1 2.0 fusion.155
  1996.3 10.9 stack.311
  2008.4 3.6 collective-permute-start.11
  2013.4 3.0 collective-permute-done.12
  2020.7 185.1 %all-to-all-start.7 = ((f32[64,6,1,256]{3,2,1,0:T(1,128)}), f32[64,6,1,256]{3,2,1,0:T(1,128)S(1)}, u32[]{:S(2)}, u32[]{:S(2)}) async-start(f32[64,6,1,256]{3,2,1,0:T(1,128)} %broadcast_in_dim.222), calls=%async_computation.7 | async-start | bytes 786432 | tf_op jit(solution)/shard_map/all_to_all | solution.py:42
  2206.5 14.5 all-to-all-done.7
  2226.8 10.4 collective-permute-start.13
  2238.7 3.1 collective-permute-done.14
  2242.7 4.8 all_to_all.88
  2248.6 13.2 all_to_all.89
  2267.7 15.1 all_to_all.90
  2285.1 3.6 collective-permute-start.15
  2290.1 2.9 collective-permute-done.16
  2295.3 5.3 all_to_all.91
  2302.6 4.1 all-to-all-start.12
  2306.7 9.1 all-to-all-done.12
  2322.3 5.8 all-to-all-start.13
  2328.2 9.5 all-to-all-done.13
  (2745 shorter events, 629.3 us)
Async XLA Ops:
  2.1 25.4 %collective-permute-start.3 = (f32[3,1,32,128]{3,2,1,0:T(8,128)S(1)}, f32[3,1,32,128]{3,2,1,0:T(8,128)S(1)}, u32[]{:S(2)}, u32[]{:S(2)}) collective-permute-start(f32[3,1,32,128]{3,2,1,0:T(8,128)S(1)} %get-tuple-element.941), channel_id=1, source_target_pairs={{0,1},{1,2},{2,3},{3,4},{4,5},{5,6},{6,7},{7,8},{8,9},{9,10},{10,1... | collective-permute-start | bytes 147464 | tf_op jit(solution)/shard_map/ppermute | solution.py:75
  5.8 21.7 collective-permute-start.1
  7.1 20.4 collective-permute-start
  11.1 17.2 collective-permute-start.2
  27.6 66.4 %copy-start.22 = (f32[8,32,128]{2,1,0:T(8,128)}, f32[8,32,128]{2,1,0:T(8,128)S(1)}, u32[]{:S(2)}) copy-start(f32[8,32,128]{2,1,0:T(8,128)S(1)} %get-tuple-element.904) | copy-start | bytes 393220
  28.5 65.7 %copy-start.23 = (f32[8,32,128]{2,1,0:T(8,128)}, f32[8,32,128]{2,1,0:T(8,128)S(1)}, u32[]{:S(2)}) copy-start(f32[8,32,128]{2,1,0:T(8,128)S(1)} %get-tuple-element.908) | copy-start | bytes 393220
  28.5 74.0 %copy-start.15 = (f32[8,32,128]{2,1,0:T(8,128)}, f32[8,32,128]{2,1,0:T(8,128)S(1)}, u32[]{:S(2)}) copy-start(f32[8,32,128]{2,1,0:T(8,128)S(1)} %get-tuple-element.906) | copy-start | bytes 393220
  28.5 74.0 %copy-start.17 = (f32[8,32,128]{2,1,0:T(8,128)}, f32[8,32,128]{2,1,0:T(8,128)S(1)}, u32[]{:S(2)}) copy-start(f32[8,32,128]{2,1,0:T(8,128)S(1)} %get-tuple-element.907) | copy-start | bytes 393220
  39.6 25.8 %all-to-all-start.1 = ((f32[32,1,768]{2,1,0:T(1,128)}), f32[32,1,768]{2,1,0:T(1,128)}, u32[]{:S(2)}, u32[]{:S(2)}) async-start(f32[32,1,768]{2,1,0:T(1,128)} %reshape.749), calls=%async_computation.1 | async-start | bytes 196608 | tf_op jit(solution)/shard_map/all_to_all | solution.py:30
  56.0 112.8 %copy-start.56 = (f32[4,16,64]{2,1,0:T(8,128)}, f32[4,16,64]{2,1,0:T(8,128)S(1)}, u32[]{:S(2)}) copy-start(f32[4,16,64]{2,1,0:T(8,128)S(1)} %broadcast_reduce_fusion.7) | copy-start | bytes 49156
  60.2 108.6 %copy-start.29 = (f32[4,16,64]{2,1,0:T(8,128)}, f32[4,16,64]{2,1,0:T(8,128)S(1)}, u32[]{:S(2)}) copy-start(f32[4,16,64]{2,1,0:T(8,128)S(1)} %get-tuple-element.1473) | copy-start | bytes 49156
  60.2 108.6 %copy-start.31 = (f32[4,16,64]{2,1,0:T(8,128)}, f32[4,16,64]{2,1,0:T(8,128)S(1)}, u32[]{:S(2)}) copy-start(f32[4,16,64]{2,1,0:T(8,128)S(1)} %broadcast_multiply_fusion.9) | copy-start | bytes 49156
  63.7 105.1 %copy-start.58 = (f32[4,16,64]{2,1,0:T(8,128)}, f32[4,16,64]{2,1,0:T(8,128)S(1)}, u32[]{:S(2)}) copy-start(f32[4,16,64]{2,1,0:T(8,128)S(1)} %get-tuple-element.1476) | copy-start | bytes 49156
  63.8 53.1 %copy-start.60 = (f32[4,16,64]{2,1,0:T(8,128)}, f32[4,16,64]{2,1,0:T(8,128)S(1)}, u32[]{:S(2)}) copy-start(f32[4,16,64]{2,1,0:T(8,128)S(1)} %get-tuple-element.1147) | copy-start | bytes 49156
  63.8 53.1 %copy-start.110 = (f32[4,16,64]{2,1,0:T(8,128)}, f32[4,16,64]{2,1,0:T(8,128)S(1)}, u32[]{:S(2)}) copy-start(f32[4,16,64]{2,1,0:T(8,128)S(1)} %get-tuple-element.1142) | copy-start | bytes 49156
  63.9 96.5 %copy-start.144 = (f32[4,16,64]{2,1,0:T(8,128)}, f32[4,16,64]{2,1,0:T(8,128)S(1)}, u32[]{:S(2)}) copy-start(f32[4,16,64]{2,1,0:T(8,128)S(1)} %get-tuple-element.1145) | copy-start | bytes 49156
  63.9 96.6 %copy-start.143 = (f32[4,16,64]{2,1,0:T(8,128)}, f32[4,16,64]{2,1,0:T(8,128)S(1)}, u32[]{:S(2)}) copy-start(f32[4,16,64]{2,1,0:T(8,128)S(1)} %get-tuple-element.1148) | copy-start | bytes 49156
  64.0 52.4 %copy-start.188 = (f32[1,16,64]{2,1,0:T(8,128)}, f32[1,16,64]{2,1,0:T(8,128)S(1)}, u32[]{:S(2)}) copy-start(f32[1,16,64]{2,1,0:T(8,128)S(1)} %get-tuple-element.818) | copy-start | bytes 12292
  64.0 52.6 %copy-start.156 = (f32[1,16,64]{2,1,0:T(8,128)}, f32[1,16,64]{2,1,0:T(8,128)S(1)}, u32[]{:S(2)}) copy-start(f32[1,16,64]{2,1,0:T(8,128)S(1)} %get-tuple-element.814) | copy-start | bytes 12292
  64.0 53.0 %copy-start.158 = (f32[1,16,64]{2,1,0:T(8,128)}, f32[1,16,64]{2,1,0:T(8,128)S(1)}, u32[]{:S(2)}) copy-start(f32[1,16,64]{2,1,0:T(8,128)S(1)} %get-tuple-element.815) | copy-start | bytes 12292
  64.0 53.0 %copy-start.160 = (f32[1,16,64]{2,1,0:T(8,128)}, f32[1,16,64]{2,1,0:T(8,128)S(1)}, u32[]{:S(2)}) copy-start(f32[1,16,64]{2,1,0:T(8,128)S(1)} %get-tuple-element.817) | copy-start | bytes 12292
  64.0 53.0 %copy-start.162 = (f32[1,16,64]{2,1,0:T(8,128)}, f32[1,16,64]{2,1,0:T(8,128)S(1)}, u32[]{:S(2)}) copy-start(f32[1,16,64]{2,1,0:T(8,128)S(1)} %get-tuple-element.819) | copy-start | bytes 12292
  64.0 53.0 %copy-start.169 = (f32[1,16,64]{2,1,0:T(8,128)}, f32[1,16,64]{2,1,0:T(8,128)S(1)}, u32[]{:S(2)}) copy-start(f32[1,16,64]{2,1,0:T(8,128)S(1)} %get-tuple-element.816) | copy-start | bytes 12292
  64.0 96.5 %copy-start.139 = (f32[1,16,64]{2,1,0:T(8,128)}, f32[1,16,64]{2,1,0:T(8,128)S(1)}, u32[]{:S(2)}) copy-start(f32[1,16,64]{2,1,0:T(8,128)S(1)} %get-tuple-element.812) | copy-start | bytes 12292
  72.9 20.1 all-to-all-start.2
  95.1 4.4 collective-permute-start.4
  98.1 4.4 collective-permute-start.5
  116.4 44.1 %copy-start.141 = (f32[1,16,64]{2,1,0:T(8,128)}, f32[1,16,64]{2,1,0:T(8,128)S(1)}, u32[]{:S(2)}) copy-start(f32[1,16,64]{2,1,0:T(8,128)S(1)} %get-tuple-element.821) | copy-start | bytes 12292
  116.6 43.9 %copy-start.164 = (f32[1,16,64]{2,1,0:T(8,128)}, f32[1,16,64]{2,1,0:T(8,128)S(1)}, u32[]{:S(2)}) copy-start(f32[1,16,64]{2,1,0:T(8,128)S(1)} %get-tuple-element.831) | copy-start | bytes 12292
  116.6 43.9 %copy-start.166 = (f32[1,16,64]{2,1,0:T(8,128)}, f32[1,16,64]{2,1,0:T(8,128)S(1)}, u32[]{:S(2)}) copy-start(f32[1,16,64]{2,1,0:T(8,128)S(1)} %get-tuple-element.834) | copy-start | bytes 12292
  116.6 43.9 %copy-start.184 = (f32[1,16,64]{2,1,0:T(8,128)}, f32[1,16,64]{2,1,0:T(8,128)S(1)}, u32[]{:S(2)}) copy-start(f32[1,16,64]{2,1,0:T(8,128)S(1)} %get-tuple-element.832) | copy-start | bytes 12292
  116.6 43.9 %copy-start.186 = (f32[1,16,64]{2,1,0:T(8,128)}, f32[1,16,64]{2,1,0:T(8,128)S(1)}, u32[]{:S(2)}) copy-start(f32[1,16,64]{2,1,0:T(8,128)S(1)} %get-tuple-element.833) | copy-start | bytes 12292
  117.0 43.5 %copy-start.171 = (f32[1,16,64]{2,1,0:T(8,128)}, f32[1,16,64]{2,1,0:T(8,128)S(1)}, u32[]{:S(2)}) copy-start(f32[1,16,64]{2,1,0:T(8,128)S(1)} %get-tuple-element.828) | copy-start | bytes 12292
  117.0 43.5 %copy-start.173 = (f32[1,16,64]{2,1,0:T(8,128)}, f32[1,16,64]{2,1,0:T(8,128)S(1)}, u32[]{:S(2)}) copy-start(f32[1,16,64]{2,1,0:T(8,128)S(1)} %get-tuple-element.829) | copy-start | bytes 12292
  117.0 43.5 %copy-start.175 = (f32[1,16,64]{2,1,0:T(8,128)}, f32[1,16,64]{2,1,0:T(8,128)S(1)}, u32[]{:S(2)}) copy-start(f32[1,16,64]{2,1,0:T(8,128)S(1)} %get-tuple-element.830) | copy-start | bytes 12292
  117.0 43.5 %copy-start.177 = (f32[1,16,64]{2,1,0:T(8,128)}, f32[1,16,64]{2,1,0:T(8,128)S(1)}, u32[]{:S(2)}) copy-start(f32[1,16,64]{2,1,0:T(8,128)S(1)} %get-tuple-element.1030) | copy-start | bytes 12292
  117.0 43.5 %copy-start.179 = (f32[1,16,64]{2,1,0:T(8,128)}, f32[1,16,64]{2,1,0:T(8,128)S(1)}, u32[]{:S(2)}) copy-start(f32[1,16,64]{2,1,0:T(8,128)S(1)} %get-tuple-element.1031) | copy-start | bytes 12292
  117.0 43.5 %copy-start.181 = (f32[1,16,64]{2,1,0:T(8,128)}, f32[1,16,64]{2,1,0:T(8,128)S(1)}, u32[]{:S(2)}) copy-start(f32[1,16,64]{2,1,0:T(8,128)S(1)} %get-tuple-element.1032) | copy-start | bytes 12292
  125.5 12.7 all-to-all-start.4
  144.6 15.5 all-to-all-start.5
  160.4 530.1 %copy-start.190 = (f32[16,64]{1,0:T(8,128)}, f32[16,64]{1,0:T(8,128)S(1)}, u32[]{:S(2)}) copy-start(f32[16,64]{1,0:T(8,128)S(1)} %multiply_bitcast_fusion.7) | copy-start | bytes 12292
  160.5 530.1 %copy-start.192 = (f32[16,64]{1,0:T(8,128)}, f32[16,64]{1,0:T(8,128)S(1)}, u32[]{:S(2)}) copy-start(f32[16,64]{1,0:T(8,128)S(1)} %multiply_bitcast_fusion.6) | copy-start | bytes 12292
  160.6 4.9 collective-permute-start.6
  164.2 4.6 collective-permute-start.7
  170.2 4.3 collective-permute-start.8
  174.6 517.2 %copy-start.11 = (f32[7,2,8,32]{3,2,1,0:T(8,128)}, f32[7,2,8,32]{3,2,1,0:T(8,128)S(1)}, u32[]{:S(2)}) copy-start(f32[7,2,8,32]{3,2,1,0:T(8,128)S(1)} %get-tuple-element.1013) | copy-start | bytes 43012
  174.6 517.2 %copy-start.13 = (f32[7,2,8,32]{3,2,1,0:T(8,128)}, f32[7,2,8,32]{3,2,1,0:T(8,128)S(1)}, u32[]{:S(2)}) copy-start(f32[7,2,8,32]{3,2,1,0:T(8,128)S(1)} %get-tuple-element.1014) | copy-start | bytes 43012
  174.6 517.2 %copy-start.25 = (f32[4,8,32]{2,1,0:T(8,128)}, f32[4,8,32]{2,1,0:T(8,128)S(1)}, u32[]{:S(2)}) copy-start(f32[4,8,32]{2,1,0:T(8,128)S(1)} %fusion.81) | copy-start | bytes 12292
  174.8 533.3 %copy-start.129 = (f32[4,8,32]{2,1,0:T(8,128)}, f32[4,8,32]{2,1,0:T(8,128)S(1)}, u32[]{:S(2)}) copy-start(f32[4,8,32]{2,1,0:T(8,128)S(1)} %get-tuple-element.1012) | copy-start | bytes 12292
  174.8 533.3 %copy-start.147 = (f32[4,8,32]{2,1,0:T(8,128)}, f32[4,8,32]{2,1,0:T(8,128)S(1)}, u32[]{:S(2)}) copy-start(f32[4,8,32]{2,1,0:T(8,128)S(1)} %get-tuple-element.787) | copy-start | bytes 12292
  716.5 252.0 %all-to-all-start.6 = ((f32[64,6,1,256]{3,2,1,0:T(1,128)}), f32[64,6,1,256]{3,2,1,0:T(1,128)}, u32[]{:S(2)}, u32[]{:S(2)}) async-start(f32[64,6,1,256]{3,2,1,0:T(1,128)} %broadcast_in_dim.193), calls=%async_computation.6 | async-start | bytes 786432 | tf_op jit(solution)/shard_map/all_to_all | solution.py:42
  1293.5 2.7 collective-permute-start.9
  1294.8 4.3 collective-permute-start.10
  1303.8 506.8 %copy-start = (f32[64,32,16]{2,1,0:T(8,128)S(1)}, f32[64,32,16]{2,1,0:T(8,128)}, u32[]{:S(2)}) copy-start(f32[64,32,16]{2,1,0:T(8,128)} %get-tuple-element.923) | copy-start | bytes 393220
  1303.8 506.8 %copy-start.7 = (f32[64,32,16]{2,1,0:T(8,128)S(1)}, f32[64,32,16]{2,1,0:T(8,128)}, u32[]{:S(2)}) copy-start(f32[64,32,16]{2,1,0:T(8,128)} %get-tuple-element.922) | copy-start | bytes 393220
  2008.4 5.0 collective-permute-start.11
  2012.0 4.3 collective-permute-start.12
  2020.7 200.2 %all-to-all-start.7 = ((f32[64,6,1,256]{3,2,1,0:T(1,128)}), f32[64,6,1,256]{3,2,1,0:T(1,128)S(1)}, u32[]{:S(2)}, u32[]{:S(2)}) async-start(f32[64,6,1,256]{3,2,1,0:T(1,128)} %broadcast_in_dim.222), calls=%async_computation.7 | async-start | bytes 786432 | tf_op jit(solution)/shard_map/all_to_all | solution.py:42
  2226.8 11.9 collective-permute-start.13
  2237.1 4.6 collective-permute-start.14
  2285.1 5.0 collective-permute-start.15
  2288.7 4.4 collective-permute-start.16
  2302.6 13.2 all-to-all-start.12
  2322.3 15.3 all-to-all-start.13
  (200 other events, 2103.3 us)

commit v2 on v0

--- a/solution.py
+++ b/solution.py
@@ -100,18 +100,47 @@
     return jnp.concatenate([edge, lax.slice_in_dim(field, 0, size - 1, axis=axis)], axis=axis)
 
 
+def pair_matrix(size, parity):
+    rows = jnp.arange(size)[:, None]
+    cols = jnp.arange(size // 2)[None, :]
+    if parity is None:
+        return (rows // 2 == cols).astype(jnp.float32)
+    return (rows == 2 * cols + parity).astype(jnp.float32)
+
+
+def coarse_pick(field, y_parity, x_parity, z_parity):
+    depth, width, height = field.shape
+    if y_parity is None:
+        picked = field[0::2] + field[1::2]
+    else:
+        picked = field[y_parity::2]
+    picked = jnp.dot(
+        picked.reshape(-1, height), pair_matrix(height, z_parity), precision=lax.Precision.HIGHEST
+    ).reshape(depth // 2, width, height // 2)
+    return jnp.einsum(
+        "xa,yxb->yab", pair_matrix(width, x_parity), picked, precision=lax.Precision.HIGHEST
+    )
+
+
 def coarse_sum(field):
+    return coarse_pick(field, None, None, None)
+
+
+def coarse_face(face, axis, parity):
+    parities = [None, None, None]
+    parities[axis] = parity
+    return 0.25 * coarse_pick(face, *parities)
+
+
+def prolong(field):
     depth, width, height = field.shape
-    return field.reshape(depth // 2, 2, width // 2, 2, height // 2, 2).sum(axis=(1, 3, 5))
-
-
-def coarse_face(face, axis, parity):
-    picked = lax.slice_in_dim(face, parity, face.shape[axis], stride=2, axis=axis)
-    return 0.125 * coarse_sum(jnp.repeat(picked, 2, axis=axis))
-
-
-def prolong(field):
-    return jnp.repeat(jnp.repeat(jnp.repeat(field, 2, axis=0), 2, axis=1), 2, axis=2)
+    grown = jnp.repeat(field, 2, axis=0)
+    grown = jnp.dot(
+        grown.reshape(-1, height), pair_matrix(2 * height, None).T, precision=lax.Precision.HIGHEST
+    ).reshape(2 * depth, width, 2 * height)
+    return jnp.einsum(
+        "xa,yab->yxb", pair_matrix(2 * width, None), grown, precision=lax.Precision.HIGHEST
+    )
 
 
 def upper_flag(bit):

time: 566 us -> 517 us (0.913)
  local copies, waits for them, and re-layouts: 103 us -> 54.9 us
  other arithmetic: 50.7 us -> 24.9 us
  waiting for transfers between devices: 178 us -> 193 us
  matrix products: 0 us -> 12.1 us
    reshape x13 -> x0, local copies, waits for them, and re-layouts: 21.8 us -> none  [the longest x5 20.9 us: coarse_sum(): field.reshape(depth // 2, 2, width // 2, 2, height // 2, 2)]
    reduce_sum x35 -> x0, other arithmetic: 14.4 us -> none  [coarse_sum(): field.reshape(depth // 2, 2, width // 2, 2, height // 2, 2)]
    dot_general x0 -> x79, matrix products: none -> 12.1 us  [the longest x35 5.38 us: coarse_pick(): jnp.dot(picked.reshape(-1, height), pair_matrix(height, z_parity), precis...]
    broadcast_in_dim x51 -> x5, local copies, waits for them, and re-layouts: 10.5 us -> 0.02 us  [prolong(): grown = jnp.repeat(field, 2, axis=0)]
    all_to_all x3, waiting for transfers between devices: 16.7 us -> 26.4 us  [turned_blocks(): lax.all_to_all(parts, axes[k], split_axis=k, concat_axis=k, tiled=True)]
    slice x33 -> x0, local copies, waits for them, and re-layouts: 8.79 us -> none  [coarse_face(): lax.slice_in_dim(face, parity, face.shape[axis], stride=2, axis=axis)]
    unnamed x286 -> x144, local copies, waits for them, and re-layouts: 15.5 us -> 13 us
  transfers between devices with their start and end apart: 44 -> 44, of which waited for: 28 -> 30; matrix products, arithmetic and copies ran while one was open for 8% -> 1% of each run, Pallas kernels for 0% -> 0%
where the time goes in v2:
time: 517 us; the launch traced here: 508 us
  waiting for transfers between devices  193 us (37%)
  starting transfers between devices  166 us (32%)
  local copies, waits for them, and re-layouts  54.9 us (11%)
  blocking collectives  47.8 us (9%)
  other arithmetic  24.9 us (5%)
  matrix products  12.1 us (2%)
  between operations  9.57 us (2%)
    all_to_all x8, waiting for transfers between devices, copy_for_each(): lax.all_to_all(jnp.broadcast_to(x[None], (count, *x.shape)), axis, 0, 0,...  98.1 us
    all_to_all x8, starting transfers between devices, copy_for_each(): lax.all_to_all(jnp.broadcast_to(x[None], (count, *x.shape)), axis, 0, 0,...  49.4 us
    ppermute x11, starting transfers between devices, padded(): lax.ppermute(head, axis, [((i + 1) % count, i) for i in range(ends)])  38.2 us
    all_to_all x5, blocking collectives, turned_blocks(): lax.all_to_all(parts, axes[k], split_axis=k, concat_axis=k, tiled=True)  32.7 us
    ppermute x11, waiting for transfers between devices, padded(): lax.ppermute(tail, axis, [(i, (i + 1) % count) for i in range(ends)])  31.2 us
    all_to_all x3, waiting for transfers between devices, reduced_moved(): lax.all_to_all(jnp.stack([prev_last, next_first]), GY, split_axis=1, conc...  28.8 us
    all_to_all x3, waiting for transfers between devices, turned_blocks(): lax.all_to_all(parts, axes[k], split_axis=k, concat_axis=k, tiled=True)  26.4 us
    all_to_all x3, starting transfers between devices, turned_blocks(): lax.all_to_all(parts, axes[k], split_axis=k, concat_axis=k, tiled=True)  23.5 us
  transfers between devices with their start and end apart: 44, of which 30 were waited for; matrix products, arithmetic and copies ran while one was open for 1% of the time, Pallas kernels for 0%

profile of v2, /device:TPU:57, one launch (start us, length us, event | category | flops | bytes accessed | tf_op | source)
XLA Modules:
  0.0 507.7 jit_solution(13546617840342689079)
XLA Ops:
  3.3 4.0 collective-permute-start
  7.4 3.1 collective-permute-start.2
  10.5 3.0 collective-permute-start.3
  19.3 3.5 all_to_all.116
  25.5 15.3 %all-to-all-start.1 = ((f32[32,1,768]{2,1,0:T(1,128)}), f32[32,1,768]{2,1,0:T(1,128)S(1)}, u32[]{:S(2)}, u32[]{:S(2)}) async-start(f32[32,1,768]{2,1,0:T(1,128)} %reshape.2578), calls=%async_computation.1 | async-start | bytes 196608 | tf_op jit(solution)/shard_map/all_to_all | solution.py:30
  41.1 8.8 %all-to-all-done.1 = f32[32,1,768]{2,1,0:T(1,128)S(1)} async-done(((f32[32,1,768]{2,1,0:T(1,128)}), f32[32,1,768]{2,1,0:T(1,128)S(1)}, u32[]{:S(2)}, u32[]{:S(2)}) %all-to-all-start.1) | async-done | bytes 98336 | tf_op jit(solution)/shard_map/all_to_all | solution.py:30
  56.6 5.8 %all-to-all-start.2 = ((f32[64,1,128]{2,1,0:T(1,128)}), f32[64,1,128]{2,1,0:T(1,128)S(1)}, u32[]{:S(2)}, u32[]{:S(2)}) async-start(f32[64,1,128]{2,1,0:T(1,128)} %reshape.2580), calls=%async_computation.2 | async-start | bytes 65536 | tf_op jit(solution)/shard_map/all_to_all | solution.py:273
  62.4 9.4 %all-to-all-done.2 = f32[64,1,128]{2,1,0:T(1,128)S(1)} async-done(((f32[64,1,128]{2,1,0:T(1,128)}), f32[64,1,128]{2,1,0:T(1,128)S(1)}, u32[]{:S(2)}, u32[]{:S(2)}) %all-to-all-start.2) | async-done | bytes 32800 | tf_op jit(solution)/shard_map/all_to_all | solution.py:273
  73.1 3.0 collective-permute-start.4
  77.5 2.9 collective-permute-done.5
  82.2 5.5 %all_to_all.117 = f32[2,1,3072]{2,1,0:T(1,128)S(1)} all-to-all(f32[2,1,3072]{2,1,0:T(1,128)S(1)} %reshape.2582), channel_id=1, replica_groups=mesh['gx'=8,'gy_0'=8,'gy_1'=4,'gy_2'=2] {'gy_2'}, dimensions={0} | all-to-all | bytes 49152 | tf_op jit(solution)/shard_map/all_to_all | solution.py:30
  89.5 4.3 all-to-all-start.4
  94.0 8.5 %all-to-all-done.4 = f32[32,1,192]{2,1,0:T(1,128)S(1)} async-done(((f32[32,1,192]{2,1,0:T(1,128)}), f32[32,1,192]{2,1,0:T(1,128)S(1)}, u32[]{:S(2)}, u32[]{:S(2)}) %all-to-all-start.4) | async-done | bytes 24608 | tf_op jit(solution)/shard_map/all_to_all | solution.py:30
  109.0 5.5 %all-to-all-start.5 = ((f32[2,64,16]{2,0,1:T(2,128)}), f32[2,64,16]{2,0,1:T(2,128)S(1)}, u32[]{:S(2)}, u32[]{:S(2)}) async-start(f32[2,64,16]{2,0,1:T(2,128)} %copy.416), calls=%async_computation.5 | async-start | bytes 131072 | tf_op jit(solution)/shard_map/all_to_all | solution.py:273
  114.7 9.9 %all-to-all-done.5 = f32[2,64,16]{2,0,1:T(2,128)S(1)} async-done(((f32[2,64,16]{2,0,1:T(2,128)}), f32[2,64,16]{2,0,1:T(2,128)S(1)}, u32[]{:S(2)}, u32[]{:S(2)}) %all-to-all-start.5) | async-done | bytes 8224 | tf_op jit(solution)/shard_map/all_to_all | solution.py:273
  125.0 3.5 collective-permute-start.6
  129.9 3.2 collective-permute-done.7
  134.4 3.5 collective-permute-start.8
  140.8 4.4 all-to-all-start.6
  145.7 14.8 %all-to-all-done.6 = f32[64,6,1,256]{3,2,1,0:T(1,128)S(1)} async-done(((f32[64,6,1,256]{3,2,1,0:T(1,128)}), f32[64,6,1,256]{3,2,1,0:T(1,128)S(1)}, u32[]{:S(2)}, u32[]{:S(2)}) %all-to-all-start.6) | async-done | bytes 393248 | tf_op jit(solution)/shard_map/all_to_all | solution.py:42
  165.6 3.6 collective-permute-start.9
  170.7 3.0 collective-permute-done.10
  174.9 2.8 collective-permute-start.11
  183.2 8.0 %all-to-all-start.7 = ((f32[64,1,384]{2,1,0:T(1,128)}), f32[64,1,384]{2,1,0:T(1,128)S(1)}, u32[]{:S(2)}, u32[]{:S(2)}) async-start(f32[64,1,384]{2,1,0:T(1,128)} %reshape.2586), calls=%async_computation.7 | async-start | bytes 196608 | tf_op jit(solution)/shard_map/all_to_all | solution.py:42
  191.3 10.4 %all-to-all-done.7 = f32[64,1,384]{2,1,0:T(1,128)S(1)} async-done(((f32[64,1,384]{2,1,0:T(1,128)}), f32[64,1,384]{2,1,0:T(1,128)S(1)}, u32[]{:S(2)}, u32[]{:S(2)}) %all-to-all-start.7) | async-done | bytes 98336 | tf_op jit(solution)/shard_map/all_to_all | solution.py:42
  206.0 3.1 collective-permute-start.12
  210.5 3.0 collective-permute-done.13
  214.8 3.0 collective-permute-start.14
  217.8 2.9 collective-permute-done.14
  223.9 7.0 %all-to-all-start.8 = ((f32[64,6,1,16]{3,2,1,0:T(1,128)}), f32[64,6,1,16]{3,2,1,0:T(1,128)S(1)}, u32[]{:S(2)}, u32[]{:S(2)}) async-start(f32[64,6,1,16]{3,2,1,0:T(1,128)} %broadcast_in_dim.49), calls=%async_computation.8 | async-start | bytes 393216 | tf_op jit(solution)/shard_map/all_to_all | solution.py:42
  231.0 12.1 %all-to-all-done.8 = f32[64,6,1,16]{3,2,1,0:T(1,128)S(1)} async-done(((f32[64,6,1,16]{3,2,1,0:T(1,128)}), f32[64,6,1,16]{3,2,1,0:T(1,128)S(1)}, u32[]{:S(2)}, u32[]{:S(2)}) %all-to-all-start.8) | async-done | bytes 24608 | tf_op jit(solution)/shard_map/all_to_all | solution.py:42
  245.5 2.9 collective-permute-start.15
  249.7 3.0 collective-permute-done.16
  253.1 2.6 collective-permute-start.17
  255.7 1.8 collective-permute-done.17
  258.5 7.0 %all-to-all-start.9 = ((f32[64,6,1,4]{1,3,2,0:T(4,128)}), f32[64,6,1,4]{1,3,2,0:T(4,128)S(1)}, u32[]{:S(2)}, u32[]{:S(2)}) async-start(f32[64,6,1,4]{1,3,2,0:T(4,128)} %broadcast_in_dim.51), calls=%async_computation.9 | async-start | bytes 262144 | tf_op jit(solution)/shard_map/all_to_all | solution.py:42
  265.5 11.3 %all-to-all-done.9 = f32[64,6,1,4]{1,3,2,0:T(4,128)S(1)} async-done(((f32[64,6,1,4]{1,3,2,0:T(4,128)}), f32[64,6,1,4]{1,3,2,0:T(4,128)S(1)}, u32[]{:S(2)}, u32[]{:S(2)}) %all-to-all-start.9) | async-done | bytes 6176 | tf_op jit(solution)/shard_map/all_to_all | solution.py:42
  280.6 4.0 collective-permute-start.18
  286.2 5.6 %all-to-all-start.10 = ((f32[64,6,1,4]{1,3,2,0:T(4,128)}), f32[64,6,1,4]{1,3,2,0:T(4,128)S(1)}, u32[]{:S(2)}, u32[]{:S(2)}) async-start(f32[64,6,1,4]{1,3,2,0:T(4,128)} %broadcast_in_dim.53), calls=%async_computation.10 | async-start | bytes 262144 | tf_op jit(solution)/shard_map/all_to_all | solution.py:42
  291.8 11.3 %all-to-all-done.10 = f32[64,6,1,4]{1,3,2,0:T(4,128)S(1)} async-done(((f32[64,6,1,4]{1,3,2,0:T(4,128)}), f32[64,6,1,4]{1,3,2,0:T(4,128)S(1)}, u32[]{:S(2)}, u32[]{:S(2)}) %all-to-all-start.10) | async-done | bytes 6176 | tf_op jit(solution)/shard_map/all_to_all | solution.py:42
  305.8 3.9 collective-permute-start.20
  311.0 3.0 collective-permute-done.21
  315.1 6.2 %all-to-all-start.11 = ((f32[64,6,1,16]{3,2,1,0:T(1,128)}), f32[64,6,1,16]{3,2,1,0:T(1,128)S(1)}, u32[]{:S(2)}, u32[]{:S(2)}) async-start(f32[64,6,1,16]{3,2,1,0:T(1,128)} %broadcast_in_dim.57), calls=%async_computation.11 | async-start | bytes 393216 | tf_op jit(solution)/shard_map/all_to_all | solution.py:42
  321.3 12.1 %all-to-all-done.11 = f32[64,6,1,16]{3,2,1,0:T(1,128)S(1)} async-done(((f32[64,6,1,16]{3,2,1,0:T(1,128)}), f32[64,6,1,16]{3,2,1,0:T(1,128)S(1)}, u32[]{:S(2)}, u32[]{:S(2)}) %all-to-all-start.11) | async-done | bytes 24608 | tf_op jit(solution)/shard_map/all_to_all | solution.py:42
  336.1 2.9 collective-permute-start.22
  340.4 4.1 collective-permute-done.23
  346.8 5.6 %all-to-all-start.12 = ((f32[64,1,384]{2,1,0:T(1,128)}), f32[64,1,384]{2,1,0:T(1,128)S(1)}, u32[]{:S(2)}, u32[]{:S(2)}) async-start(f32[64,1,384]{2,1,0:T(1,128)} %reshape.2588), calls=%async_computation.12 | async-start | bytes 196608 | tf_op jit(solution)/shard_map/all_to_all | solution.py:42
  352.5 10.7 %all-to-all-done.12 = f32[64,1,384]{2,1,0:T(1,128)S(1)} async-done(((f32[64,1,384]{2,1,0:T(1,128)}), f32[64,1,384]{2,1,0:T(1,128)S(1)}, u32[]{:S(2)}, u32[]{:S(2)}) %all-to-all-start.12) | async-done | bytes 98336 | tf_op jit(solution)/shard_map/all_to_all | solution.py:42
  367.8 4.8 collective-permute-start.24
  374.0 3.2 collective-permute-done.25
  378.5 5.6 %all-to-all-start.13 = ((f32[64,6,1,256]{3,2,1,0:T(1,128)}), f32[64,6,1,256]{3,2,1,0:T(1,128)S(1)}, u32[]{:S(2)}, u32[]{:S(2)}) async-start(f32[64,6,1,256]{3,2,1,0:T(1,128)} %broadcast_in_dim.63), calls=%async_computation.13 | async-start | bytes 786432 | tf_op jit(solution)/shard_map/all_to_all | solution.py:42
  384.2 15.3 %all-to-all-done.13 = f32[64,6,1,256]{3,2,1,0:T(1,128)S(1)} async-done(((f32[64,6,1,256]{3,2,1,0:T(1,128)}), f32[64,6,1,256]{3,2,1,0:T(1,128)S(1)}, u32[]{:S(2)}, u32[]{:S(2)}) %all-to-all-start.13) | async-done | bytes 393248 | tf_op jit(solution)/shard_map/all_to_all | solution.py:42
  404.9 3.6 collective-permute-start.26
  409.9 3.0 collective-permute-done.27
  413.7 5.0 all_to_all.118
  420.0 13.4 %all_to_all.119 = f32[32,1,192]{2,1,0:T(1,128)S(1)} all-to-all(f32[32,1,192]{2,1,0:T(1,128)S(1)} %reshape.2592), channel_id=1, replica_groups=mesh['gx'=8,'gy_0'=8,'gy_1'=4,'gy_2'=2] {'gy_0','gy_1'}, dimensions={0} | all-to-all | bytes 49152 | tf_op jit(solution)/shard_map/all_to_all | solution.py:30
  439.3 15.1 %all_to_all.120 = f32[2,64,16]{2,0,1:T(2,128)S(1)} all-to-all(f32[2,64,16]{2,0,1:T(2,128)S(1)} %copy.488), channel_id=1, replica_groups=mesh['gx'=8,'gy_0'=8,'gy_1'=4,'gy_2'=2] {'gy_0','gy_1','gy_2'}, dimensions={1} | all-to-all | bytes 16384 | tf_op jit(solution)/shard_map/all_to_all | solution.py:273
  455.2 2.9 collective-permute-start.28
  459.5 2.9 collective-permute-done.29
  463.1 5.3 %all_to_all.121 = f32[2,1,12288]{2,1,0:T(1,128)S(1)} all-to-all(f32[2,1,12288]{2,1,0:T(1,128)S(1)} %reshape.2594), channel_id=1, replica_groups=mesh['gx'=8,'gy_0'=8,'gy_1'=4,'gy_2'=2] {'gy_2'}, dimensions={0} | all-to-all | bytes 196608 | tf_op jit(solution)/shard_map/all_to_all | solution.py:30
  470.5 3.9 all-to-all-start.18
  474.4 9.1 %all-to-all-done.18 = f32[32,1,768]{2,1,0:T(1,128)S(1)} async-done(((f32[32,1,768]{2,1,0:T(1,128)}), f32[32,1,768]{2,1,0:T(1,128)S(1)}, u32[]{:S(2)}, u32[]{:S(2)}) %all-to-all-start.18) | async-done | bytes 98336 | tf_op jit(solution)/shard_map/all_to_all | solution.py:30
  490.2 5.8 %all-to-all-start.19 = ((f32[64,1,128]{2,1,0:T(1,128)}), f32[64,1,128]{2,1,0:T(1,128)S(1)}, u32[]{:S(2)}, u32[]{:S(2)}) async-start(f32[64,1,128]{2,1,0:T(1,128)} %reshape.2598), calls=%async_computation.19 | async-start | bytes 65536 | tf_op jit(solution)/shard_map/all_to_all | solution.py:273
  496.0 9.4 %all-to-all-done.19 = f32[64,1,128]{2,1,0:T(1,128)S(1)} async-done(((f32[64,1,128]{2,1,0:T(1,128)}), f32[64,1,128]{2,1,0:T(1,128)S(1)}, u32[]{:S(2)}, u32[]{:S(2)}) %all-to-all-start.19) | async-done | bytes 32800 | tf_op jit(solution)/shard_map/all_to_all | solution.py:273
  (2815 shorter events, 111.0 us)
Async XLA Ops:
  1.0 0.9 copy-start.1
  1.0 1.0 copy-start.2
  2.0 12.2 %collective-permute-start.1 = (f32[3,8,1,128]{3,2,1,0:T(1,128)S(1)}, f32[3,8,1,128]{3,2,1,0:T(1,128)S(1)}, u32[]{:S(2)}, u32[]{:S(2)}) collective-permute-start(f32[3,8,1,128]{3,2,1,0:T(1,128)S(1)} %get-tuple-element.611), channel_id=1, source_target_pairs={{0,64},{64,128},{128,192},{192,256},{256,320},{320,384},{384,448},... | collective-permute-start | bytes 36872 | tf_op jit(solution)/shard_map/ppermute | solution.py:75
  3.3 10.9 %collective-permute-start = (f32[3,8,1,128]{3,2,1,0:T(1,128)S(1)}, f32[3,8,1,128]{3,2,1,0:T(1,128)S(1)}, u32[]{:S(2)}, u32[]{:S(2)}) collective-permute-start(f32[3,8,1,128]{3,2,1,0:T(1,128)S(1)} %get-tuple-element.612), channel_id=1, source_target_pairs={{64,0},{128,64},{192,128},{256,192},{320,256},{384,320},{448,384},... | collective-permute-start | bytes 36872 | tf_op jit(solution)/shard_map/ppermute | solution.py:76
  7.4 8.0 %collective-permute-start.2 = (f32[3,1,32,128]{3,2,1,0:T(8,128)S(1)}, f32[3,1,32,128]{3,2,1,0:T(8,128)S(1)}, u32[]{:S(2)}, u32[]{:S(2)}) collective-permute-start(f32[3,1,32,128]{3,2,1,0:T(8,128)S(1)} %get-tuple-element.609), channel_id=1, source_target_pairs={{1,0},{2,1},{3,2},{4,3},{5,4},{6,5},{7,6},{8,7},{9,8},{10,9},{11,1... | collective-permute-start | bytes 147464 | tf_op jit(solution)/shard_map/ppermute | solution.py:76
  10.5 4.2 collective-permute-start.3
  14.2 0.9 copy-start.3
  15.1 0.9 copy-start
  25.5 24.4 %all-to-all-start.1 = ((f32[32,1,768]{2,1,0:T(1,128)}), f32[32,1,768]{2,1,0:T(1,128)S(1)}, u32[]{:S(2)}, u32[]{:S(2)}) async-start(f32[32,1,768]{2,1,0:T(1,128)} %reshape.2578), calls=%async_computation.1 | async-start | bytes 196608 | tf_op jit(solution)/shard_map/all_to_all | solution.py:30
  56.6 15.2 %all-to-all-start.2 = ((f32[64,1,128]{2,1,0:T(1,128)}), f32[64,1,128]{2,1,0:T(1,128)S(1)}, u32[]{:S(2)}, u32[]{:S(2)}) async-start(f32[64,1,128]{2,1,0:T(1,128)} %reshape.2580), calls=%async_computation.2 | async-start | bytes 65536 | tf_op jit(solution)/shard_map/all_to_all | solution.py:273
  73.1 4.4 collective-permute-start.4
  76.1 4.4 collective-permute-start.5
  89.5 13.0 %all-to-all-start.4 = ((f32[32,1,192]{2,1,0:T(1,128)}), f32[32,1,192]{2,1,0:T(1,128)S(1)}, u32[]{:S(2)}, u32[]{:S(2)}) async-start(f32[32,1,192]{2,1,0:T(1,128)} %reshape.2584), calls=%async_computation.4 | async-start | bytes 65536 | tf_op jit(solution)/shard_map/all_to_all | solution.py:30
  109.0 15.6 %all-to-all-start.5 = ((f32[2,64,16]{2,0,1:T(2,128)}), f32[2,64,16]{2,0,1:T(2,128)S(1)}, u32[]{:S(2)}, u32[]{:S(2)}) async-start(f32[2,64,16]{2,0,1:T(2,128)} %copy.416), calls=%async_computation.5 | async-start | bytes 131072 | tf_op jit(solution)/shard_map/all_to_all | solution.py:273
  125.0 4.9 collective-permute-start.6
  128.5 4.6 collective-permute-start.7
  134.4 4.3 collective-permute-start.8
  140.8 19.8 %all-to-all-start.6 = ((f32[64,6,1,256]{3,2,1,0:T(1,128)}), f32[64,6,1,256]{3,2,1,0:T(1,128)S(1)}, u32[]{:S(2)}, u32[]{:S(2)}) async-start(f32[64,6,1,256]{3,2,1,0:T(1,128)} %broadcast_in_dim.45), calls=%async_computation.6 | async-start | bytes 786432 | tf_op jit(solution)/shard_map/all_to_all | solution.py:42
  165.6 5.0 collective-permute-start.9
  169.3 4.3 collective-permute-start.10
  174.9 4.6 collective-permute-start.11
  183.2 18.6 %all-to-all-start.7 = ((f32[64,1,384]{2,1,0:T(1,128)}), f32[64,1,384]{2,1,0:T(1,128)S(1)}, u32[]{:S(2)}, u32[]{:S(2)}) async-start(f32[64,1,384]{2,1,0:T(1,128)} %reshape.2586), calls=%async_computation.7 | async-start | bytes 196608 | tf_op jit(solution)/shard_map/all_to_all | solution.py:42
  206.0 4.5 collective-permute-start.12
  209.1 4.3 collective-permute-start.13
  214.8 6.0 %collective-permute-start.14 = (f32[7,2,2,8]{3,2,1,0:T(2,128)S(1)}, f32[7,2,2,8]{3,2,1,0:T(2,128)S(1)}, u32[]{:S(2)}, u32[]{:S(2)}) collective-permute-start(f32[7,2,2,8]{3,2,1,0:T(2,128)S(1)} %fusion.40), channel_id=1, source_target_pairs={{0,4},{1,5},{2,6},{3,7},{4,0},{5,1},{6,2},{7,3},{8,12},{9,13},{10,... | collective-permute-start | bytes 2696 | tf_op jit(solution)/shard_map/ppermute | solution.py:88
  223.9 19.3 %all-to-all-start.8 = ((f32[64,6,1,16]{3,2,1,0:T(1,128)}), f32[64,6,1,16]{3,2,1,0:T(1,128)S(1)}, u32[]{:S(2)}, u32[]{:S(2)}) async-start(f32[64,6,1,16]{3,2,1,0:T(1,128)} %broadcast_in_dim.49), calls=%async_computation.8 | async-start | bytes 393216 | tf_op jit(solution)/shard_map/all_to_all | solution.py:42
  245.5 4.2 collective-permute-start.15
  248.3 4.3 collective-permute-start.16
  253.1 4.4 collective-permute-start.17
  258.5 18.4 %all-to-all-start.9 = ((f32[64,6,1,4]{1,3,2,0:T(4,128)}), f32[64,6,1,4]{1,3,2,0:T(4,128)S(1)}, u32[]{:S(2)}, u32[]{:S(2)}) async-start(f32[64,6,1,4]{1,3,2,0:T(4,128)} %broadcast_in_dim.51), calls=%async_computation.9 | async-start | bytes 262144 | tf_op jit(solution)/shard_map/all_to_all | solution.py:42
  279.3 5.3 %collective-permute-start.19 = (f32[4,1,4]{2,0,1:T(4,128)S(1)}, f32[4,1,4]{2,0,1:T(4,128)S(1)}, u32[]{:S(2)}, u32[]{:S(2)}) collective-permute-start(f32[4,1,4]{2,0,1:T(4,128)S(1)} %fusion.452), channel_id=1, source_target_pairs={{0,64},{64,128},{128,192},{192,256},{256,320},{320,384},{384,448},... | collective-permute-start | bytes 200 | tf_op jit(solution)/shard_map/ppermute | solution.py:58
  280.6 4.7 collective-permute-start.18
  286.2 16.9 %all-to-all-start.10 = ((f32[64,6,1,4]{1,3,2,0:T(4,128)}), f32[64,6,1,4]{1,3,2,0:T(4,128)S(1)}, u32[]{:S(2)}, u32[]{:S(2)}) async-start(f32[64,6,1,4]{1,3,2,0:T(4,128)} %broadcast_in_dim.53), calls=%async_computation.10 | async-start | bytes 262144 | tf_op jit(solution)/shard_map/all_to_all | solution.py:42
  305.8 5.3 %collective-permute-start.20 = (f32[4,1,8]{2,1,0:T(1,128)S(1)}, f32[4,1,8]{2,1,0:T(1,128)S(1)}, u32[]{:S(2)}, u32[]{:S(2)}) collective-permute-start(f32[4,1,8]{2,1,0:T(1,128)S(1)} %get-tuple-element.1192), channel_id=1, source_target_pairs={{64,0},{128,64},{192,128},{256,192},{320,256},{384,320},{448,384},... | collective-permute-start | bytes 392 | tf_op jit(solution)/shard_map/ppermute | solution.py:60
  309.7 4.3 collective-permute-start.21
  315.1 18.3 %all-to-all-start.11 = ((f32[64,6,1,16]{3,2,1,0:T(1,128)}), f32[64,6,1,16]{3,2,1,0:T(1,128)S(1)}, u32[]{:S(2)}, u32[]{:S(2)}) async-start(f32[64,6,1,16]{3,2,1,0:T(1,128)} %broadcast_in_dim.57), calls=%async_computation.11 | async-start | bytes 393216 | tf_op jit(solution)/shard_map/all_to_all | solution.py:42
  336.1 4.2 collective-permute-start.22
  339.0 5.5 %collective-permute-start.23 = (f32[4,1,16]{2,1,0:T(1,128)S(1)}, f32[4,1,16]{2,1,0:T(1,128)S(1)}, u32[]{:S(2)}, u32[]{:S(2)}) collective-permute-start(f32[4,1,16]{2,1,0:T(1,128)S(1)} %get-tuple-element.1069), channel_id=1, source_target_pairs={{0,64},{64,128},{128,192},{192,256},{256,320},{320,384},{384,448},... | collective-permute-start | bytes 776 | tf_op jit(solution)/shard_map/ppermute | solution.py:58
  346.8 16.3 %all-to-all-start.12 = ((f32[64,1,384]{2,1,0:T(1,128)}), f32[64,1,384]{2,1,0:T(1,128)S(1)}, u32[]{:S(2)}, u32[]{:S(2)}) async-start(f32[64,1,384]{2,1,0:T(1,128)} %reshape.2588), calls=%async_computation.12 | async-start | bytes 196608 | tf_op jit(solution)/shard_map/all_to_all | solution.py:42
  367.8 6.2 %collective-permute-start.24 = (f32[4,1,32]{2,1,0:T(1,128)S(1)}, f32[4,1,32]{2,1,0:T(1,128)S(1)}, u32[]{:S(2)}, u32[]{:S(2)}) collective-permute-start(f32[4,1,32]{2,1,0:T(1,128)S(1)} %get-tuple-element.945), channel_id=1, source_target_pairs={{64,0},{128,64},{192,128},{256,192},{320,256},{384,320},{448,384},... | collective-permute-start | bytes 1544 | tf_op jit(solution)/shard_map/ppermute | solution.py:60
  372.6 4.6 collective-permute-start.25
  378.5 20.9 %all-to-all-start.13 = ((f32[64,6,1,256]{3,2,1,0:T(1,128)}), f32[64,6,1,256]{3,2,1,0:T(1,128)S(1)}, u32[]{:S(2)}, u32[]{:S(2)}) async-start(f32[64,6,1,256]{3,2,1,0:T(1,128)} %broadcast_in_dim.63), calls=%async_computation.13 | async-start | bytes 786432 | tf_op jit(solution)/shard_map/all_to_all | solution.py:42
  404.9 5.0 collective-permute-start.26
  408.6 4.3 collective-permute-start.27
  455.2 4.3 collective-permute-start.28
  458.1 4.4 collective-permute-start.29
  470.5 13.0 %all-to-all-start.18 = ((f32[32,1,768]{2,1,0:T(1,128)}), f32[32,1,768]{2,1,0:T(1,128)S(1)}, u32[]{:S(2)}, u32[]{:S(2)}) async-start(f32[32,1,768]{2,1,0:T(1,128)} %reshape.2596), calls=%async_computation.18 | async-start | bytes 196608 | tf_op jit(solution)/shard_map/all_to_all | solution.py:30
  490.2 15.2 %all-to-all-start.19 = ((f32[64,1,128]{2,1,0:T(1,128)}), f32[64,1,128]{2,1,0:T(1,128)S(1)}, u32[]{:S(2)}, u32[]{:S(2)}) async-start(f32[64,1,128]{2,1,0:T(1,128)} %reshape.2598), calls=%async_computation.19 | async-start | bytes 65536 | tf_op jit(solution)/shard_map/all_to_all | solution.py:273

commit v3 on v2

--- a/solution.py
+++ b/solution.py
@@ -266,7 +266,8 @@
         [level["alpha"], level["beta"], level["gamma"], level["delta"], head, tail]
     ).reshape(6, 1, -1)
     if group == 1:
-        moved = exchange_by_chip(packed, (("gy_0", "gy_1"), "gy_2"), (1, 0), 2, 1)
+        parts = in_blocks(packed, 2, lax.axis_size(GY))
+        moved = in_order(lax.all_to_all(parts, GY, 0, 0, tiled=True), 1)
         prev_last, next_first = reduced_local(
             moved[0], moved[1], moved[2], moved[3], moved[4], moved[5]
         )

time: 517 us -> 530 us (1.025)
  local copies, waits for them, and re-layouts: 54.9 us -> 70.7 us
  blocking collectives: 47.8 us -> 33 us
  matrix products: 12.1 us -> 20 us
    unnamed x144 -> x230, local copies, waits for them, and re-layouts: 13 us -> 28.9 us
    all_to_all x5 -> x1, blocking collectives: 32.7 us -> 18.6 us  [reduced_moved(): moved = in_order(lax.all_to_all(parts, GY, 0, 0, tiled=True), 1)]
    all_to_all x3, waiting for transfers between devices: 26.4 us -> 32.9 us  [reduced_moved(): moved = in_order(lax.all_to_all(parts, GY, 0, 0, tiled=True), 1)]
  transfers between devices with their start and end apart: 44 -> 44, of which waited for: 30 -> 29; matrix products, arithmetic and copies ran while one was open for 1% -> 2% of each run, Pallas kernels for 0% -> 0%
where the time goes in v3:
time: 530 us; the launch traced here: 520 us
  waiting for transfers between devices  195 us (37%)
  starting transfers between devices  165 us (31%)
  local copies, waits for them, and re-layouts  70.7 us (13%)
  blocking collectives  33 us (6%)
  other arithmetic  26.4 us (5%)
  matrix products  20 us (4%)
  between operations  9.05 us (2%)
    all_to_all x8, waiting for transfers between devices, copy_for_each(): lax.all_to_all(jnp.broadcast_to(x[None], (count, *x.shape)), axis, 0, 0,...  95.2 us
    all_to_all x8, starting transfers between devices, copy_for_each(): lax.all_to_all(jnp.broadcast_to(x[None], (count, *x.shape)), axis, 0, 0,...  49.5 us
    ppermute x11, starting transfers between devices, padded(): lax.ppermute(head, axis, [((i + 1) % count, i) for i in range(ends)])  38.2 us
    all_to_all x3, waiting for transfers between devices, reduced_moved(): moved = in_order(lax.all_to_all(parts, GY, 0, 0, tiled=True), 1)  32.9 us
    ppermute x11, waiting for transfers between devices, padded(): lax.ppermute(tail, axis, [(i, (i + 1) % count) for i in range(ends)])  31.2 us
    unnamed x230, local copies, waits for them, and re-layouts  28.9 us
    all_to_all x3, waiting for transfers between devices, reduced_moved(): lax.all_to_all(jnp.stack([prev_last, next_first]), GY, split_axis=1, conc...  28.8 us
    all_to_all x3, starting transfers between devices, reduced_moved(): moved = in_order(lax.all_to_all(parts, GY, 0, 0, tiled=True), 1)  27 us
  transfers between devices with their start and end apart: 44, of which 29 were waited for; matrix products, arithmetic and copies ran while one was open for 2% of the time, Pallas kernels for 0%

profile of v3, /device:TPU:57, one launch (start us, length us, event | category | flops | bytes accessed | tf_op | source)
XLA Modules:
  0.0 519.8 jit_solution(14589981584014523492)
XLA Ops:
  2.0 1.3 collective-permute-start.1
  3.3 4.0 collective-permute-start
  7.4 3.1 collective-permute-start.2
  10.5 3.0 collective-permute-start.3
  23.7 14.7 %all-to-all-start = ((f32[64,1,384]{2,1,0:T(1,128)}), f32[64,1,384]{2,1,0:T(1,128)S(1)}, u32[]{:S(2)}, u32[]{:S(2)}) async-start(f32[64,1,384]{2,1,0:T(1,128)} %reshape.2544), calls=%async_computation | async-start | bytes 196608 | tf_op jit(solution)/shard_map/all_to_all | solution.py:270
  38.7 10.3 %all-to-all-done = f32[64,1,384]{2,1,0:T(1,128)S(1)} async-done(((f32[64,1,384]{2,1,0:T(1,128)}), f32[64,1,384]{2,1,0:T(1,128)S(1)}, u32[]{:S(2)}, u32[]{:S(2)}) %all-to-all-start) | async-done | bytes 98336 | tf_op jit(solution)/shard_map/all_to_all | solution.py:270
  55.6 4.4 all-to-all-start.1
  60.1 9.4 %all-to-all-done.1 = f32[64,1,128]{2,1,0:T(1,128)S(1)} async-done(((f32[64,1,128]{2,1,0:T(1,128)}), f32[64,1,128]{2,1,0:T(1,128)S(1)}, u32[]{:S(2)}, u32[]{:S(2)}) %all-to-all-start.1) | async-done | bytes 32800 | tf_op jit(solution)/shard_map/all_to_all | solution.py:274
  70.6 3.0 collective-permute-start.4
  73.6 1.3 collective-permute-start.5
  75.0 2.9 collective-permute-done.5
  79.9 6.4 %all-to-all-start.2 = ((f32[64,6,1,16]{3,2,1,0:T(1,128)}), f32[64,6,1,16]{3,2,1,0:T(1,128)S(1)}, u32[]{:S(2)}, u32[]{:S(2)}) async-start(f32[64,6,1,16]{3,2,1,0:T(1,128)} %copy.294), calls=%async_computation.2 | async-start | bytes 393216 | tf_op jit(solution)/shard_map/all_to_all | solution.py:270
  86.4 12.0 %all-to-all-done.2 = f32[64,6,1,16]{3,2,1,0:T(1,128)S(1)} async-done(((f32[64,6,1,16]{3,2,1,0:T(1,128)}), f32[64,6,1,16]{3,2,1,0:T(1,128)S(1)}, u32[]{:S(2)}, u32[]{:S(2)}) %all-to-all-start.2) | async-done | bytes 24608 | tf_op jit(solution)/shard_map/all_to_all | solution.py:270
  103.9 4.4 all-to-all-start.3
  108.6 9.9 %all-to-all-done.3 = f32[2,64,16]{2,0,1:T(2,128)S(1)} async-done(((f32[2,64,16]{2,0,1:T(2,128)}), f32[2,64,16]{2,0,1:T(2,128)S(1)}, u32[]{:S(2)}, u32[]{:S(2)}) %all-to-all-start.3) | async-done | bytes 8224 | tf_op jit(solution)/shard_map/all_to_all | solution.py:274
  118.9 3.5 collective-permute-start.6
  122.4 1.3 collective-permute-start.7
  123.8 3.2 collective-permute-done.7
  128.3 3.5 collective-permute-start.8
  138.1 4.4 all-to-all-start.4
  145.5 12.4 %all-to-all-done.4 = f32[64,6,1,256]{3,2,1,0:T(1,128)S(1)} async-done(((f32[64,6,1,256]{3,2,1,0:T(1,128)}), f32[64,6,1,256]{3,2,1,0:T(1,128)S(1)}, u32[]{:S(2)}, u32[]{:S(2)}) %all-to-all-start.4) | async-done | bytes 393248 | tf_op jit(solution)/shard_map/all_to_all | solution.py:42
  165.6 3.6 collective-permute-start.9
  170.6 3.0 collective-permute-done.10
  178.6 2.8 collective-permute-start.11
  188.5 8.0 %all-to-all-start.5 = ((f32[64,1,384]{2,1,0:T(1,128)}), f32[64,1,384]{2,1,0:T(1,128)S(1)}, u32[]{:S(2)}, u32[]{:S(2)}) async-start(f32[64,1,384]{2,1,0:T(1,128)} %reshape.2548), calls=%async_computation.5 | async-start | bytes 196608 | tf_op jit(solution)/shard_map/all_to_all | solution.py:42
  196.7 10.4 %all-to-all-done.5 = f32[64,1,384]{2,1,0:T(1,128)S(1)} async-done(((f32[64,1,384]{2,1,0:T(1,128)}), f32[64,1,384]{2,1,0:T(1,128)S(1)}, u32[]{:S(2)}, u32[]{:S(2)}) %all-to-all-start.5) | async-done | bytes 98336 | tf_op jit(solution)/shard_map/all_to_all | solution.py:42
  211.2 3.1 collective-permute-start.12
  215.7 3.0 collective-permute-done.13
  222.0 3.0 collective-permute-start.14
  225.0 2.9 collective-permute-done.14
  235.5 7.0 %all-to-all-start.6 = ((f32[64,6,1,16]{3,2,1,0:T(1,128)}), f32[64,6,1,16]{3,2,1,0:T(1,128)S(1)}, u32[]{:S(2)}, u32[]{:S(2)}) async-start(f32[64,6,1,16]{3,2,1,0:T(1,128)} %broadcast_in_dim.49), calls=%async_computation.6 | async-start | bytes 393216 | tf_op jit(solution)/shard_map/all_to_all | solution.py:42
  243.3 11.5 %all-to-all-done.6 = f32[64,6,1,16]{3,2,1,0:T(1,128)S(1)} async-done(((f32[64,6,1,16]{3,2,1,0:T(1,128)}), f32[64,6,1,16]{3,2,1,0:T(1,128)S(1)}, u32[]{:S(2)}, u32[]{:S(2)}) %all-to-all-start.6) | async-done | bytes 24608 | tf_op jit(solution)/shard_map/all_to_all | solution.py:42
  257.8 2.9 collective-permute-start.15
  262.1 3.0 collective-permute-done.16
  269.3 2.5 collective-permute-start.17
  271.9 1.8 collective-permute-done.17
  274.7 7.0 %all-to-all-start.7 = ((f32[64,6,1,4]{1,3,2,0:T(4,128)}), f32[64,6,1,4]{1,3,2,0:T(4,128)S(1)}, u32[]{:S(2)}, u32[]{:S(2)}) async-start(f32[64,6,1,4]{1,3,2,0:T(4,128)} %broadcast_in_dim.51), calls=%async_computation.7 | async-start | bytes 262144 | tf_op jit(solution)/shard_map/all_to_all | solution.py:42
  281.7 11.3 %all-to-all-done.7 = f32[64,6,1,4]{1,3,2,0:T(4,128)S(1)} async-done(((f32[64,6,1,4]{1,3,2,0:T(4,128)}), f32[64,6,1,4]{1,3,2,0:T(4,128)S(1)}, u32[]{:S(2)}, u32[]{:S(2)}) %all-to-all-start.7) | async-done | bytes 6176 | tf_op jit(solution)/shard_map/all_to_all | solution.py:42
  296.8 4.0 collective-permute-start.18
  302.4 5.6 %all-to-all-start.8 = ((f32[64,6,1,4]{1,3,2,0:T(4,128)}), f32[64,6,1,4]{1,3,2,0:T(4,128)S(1)}, u32[]{:S(2)}, u32[]{:S(2)}) async-start(f32[64,6,1,4]{1,3,2,0:T(4,128)} %broadcast_in_dim.53), calls=%async_computation.8 | async-start | bytes 262144 | tf_op jit(solution)/shard_map/all_to_all | solution.py:42
  308.0 11.3 %all-to-all-done.8 = f32[64,6,1,4]{1,3,2,0:T(4,128)S(1)} async-done(((f32[64,6,1,4]{1,3,2,0:T(4,128)}), f32[64,6,1,4]{1,3,2,0:T(4,128)S(1)}, u32[]{:S(2)}, u32[]{:S(2)}) %all-to-all-start.8) | async-done | bytes 6176 | tf_op jit(solution)/shard_map/all_to_all | solution.py:42
  321.9 3.9 collective-permute-start.20
  325.9 1.3 collective-permute-start.21
  327.2 3.0 collective-permute-done.21
  331.3 6.3 %all-to-all-start.9 = ((f32[64,6,1,16]{3,2,1,0:T(1,128)}), f32[64,6,1,16]{3,2,1,0:T(1,128)S(1)}, u32[]{:S(2)}, u32[]{:S(2)}) async-start(f32[64,6,1,16]{3,2,1,0:T(1,128)} %broadcast_in_dim.57), calls=%async_computation.9 | async-start | bytes 393216 | tf_op jit(solution)/shard_map/all_to_all | solution.py:42
  337.6 12.2 %all-to-all-done.9 = f32[64,6,1,16]{3,2,1,0:T(1,128)S(1)} async-done(((f32[64,6,1,16]{3,2,1,0:T(1,128)}), f32[64,6,1,16]{3,2,1,0:T(1,128)S(1)}, u32[]{:S(2)}, u32[]{:S(2)}) %all-to-all-start.9) | async-done | bytes 24608 | tf_op jit(solution)/shard_map/all_to_all | solution.py:42
  352.5 2.9 collective-permute-start.22
  356.7 4.1 collective-permute-done.23
  363.1 5.6 %all-to-all-start.10 = ((f32[64,1,384]{2,1,0:T(1,128)}), f32[64,1,384]{2,1,0:T(1,128)S(1)}, u32[]{:S(2)}, u32[]{:S(2)}) async-start(f32[64,1,384]{2,1,0:T(1,128)} %reshape.2550), calls=%async_computation.10 | async-start | bytes 196608 | tf_op jit(solution)/shard_map/all_to_all | solution.py:42
  368.7 10.7 %all-to-all-done.10 = f32[64,1,384]{2,1,0:T(1,128)S(1)} async-done(((f32[64,1,384]{2,1,0:T(1,128)}), f32[64,1,384]{2,1,0:T(1,128)S(1)}, u32[]{:S(2)}, u32[]{:S(2)}) %all-to-all-start.10) | async-done | bytes 98336 | tf_op jit(solution)/shard_map/all_to_all | solution.py:42
  383.9 4.8 collective-permute-start.24
  390.1 3.2 collective-permute-done.25
  395.8 5.6 %all-to-all-start.11 = ((f32[64,6,1,256]{3,2,1,0:T(1,128)}), f32[64,6,1,256]{3,2,1,0:T(1,128)S(1)}, u32[]{:S(2)}, u32[]{:S(2)}) async-start(f32[64,6,1,256]{3,2,1,0:T(1,128)} %broadcast_in_dim.63), calls=%async_computation.11 | async-start | bytes 786432 | tf_op jit(solution)/shard_map/all_to_all | solution.py:42
  401.4 15.3 %all-to-all-done.11 = f32[64,6,1,256]{3,2,1,0:T(1,128)S(1)} async-done(((f32[64,6,1,256]{3,2,1,0:T(1,128)}), f32[64,6,1,256]{3,2,1,0:T(1,128)S(1)}, u32[]{:S(2)}, u32[]{:S(2)}) %all-to-all-start.11) | async-done | bytes 393248 | tf_op jit(solution)/shard_map/all_to_all | solution.py:42
  423.5 3.6 collective-permute-start.26
  428.5 3.0 collective-permute-done.27
  432.0 18.6 %all_to_all.96 = f32[64,6,1,16]{3,2,1,0:T(1,128)S(1)} all-to-all(f32[64,6,1,16]{3,2,1,0:T(1,128)S(1)} %copy.361), channel_id=1, replica_groups=mesh['gx'=8,'gy_0'=8,'gy_1'=4,'gy_2'=2] {'gy_0','gy_1','gy_2'}, dimensions={0} | all-to-all | bytes 49152 | tf_op jit(solution)/shard_map/all_to_all | solution.py:270
  455.4 14.4 %all_to_all.97 = f32[2,64,16]{2,0,1:T(2,128)S(1)} all-to-all(f32[2,64,16]{2,0,1:T(2,128)S(1)} %copy.363), channel_id=1, replica_groups=mesh['gx'=8,'gy_0'=8,'gy_1'=4,'gy_2'=2] {'gy_0','gy_1','gy_2'}, dimensions={1} | all-to-all | bytes 16384 | tf_op jit(solution)/shard_map/all_to_all | solution.py:274
  471.2 2.9 collective-permute-start.28
  475.5 2.9 collective-permute-done.29
  480.8 5.9 %all-to-all-start.14 = ((f32[64,1,384]{2,1,0:T(1,128)}), f32[64,1,384]{2,1,0:T(1,128)S(1)}, u32[]{:S(2)}, u32[]{:S(2)}) async-start(f32[64,1,384]{2,1,0:T(1,128)} %reshape.2552), calls=%async_computation.14 | async-start | bytes 196608 | tf_op jit(solution)/shard_map/all_to_all | solution.py:270
  486.7 10.7 %all-to-all-done.14 = f32[64,1,384]{2,1,0:T(1,128)S(1)} async-done(((f32[64,1,384]{2,1,0:T(1,128)}), f32[64,1,384]{2,1,0:T(1,128)S(1)}, u32[]{:S(2)}, u32[]{:S(2)}) %all-to-all-start.14) | async-done | bytes 98336 | tf_op jit(solution)/shard_map/all_to_all | solution.py:270
  503.9 4.4 all-to-all-start.15
  508.4 9.4 %all-to-all-done.15 = f32[64,1,128]{2,1,0:T(1,128)S(1)} async-done(((f32[64,1,128]{2,1,0:T(1,128)}), f32[64,1,128]{2,1,0:T(1,128)S(1)}, u32[]{:S(2)}, u32[]{:S(2)}) %all-to-all-start.15) | async-done | bytes 32800 | tf_op jit(solution)/shard_map/all_to_all | solution.py:274
  (2873 shorter events, 129.8 us)
Async XLA Ops:
  1.0 0.9 copy-start.1
  1.0 1.0 copy-start.2
  2.0 14.4 %collective-permute-start.1 = (f32[3,8,1,128]{3,2,1,0:T(1,128)S(1)}, f32[3,8,1,128]{3,2,1,0:T(1,128)S(1)}, u32[]{:S(2)}, u32[]{:S(2)}) collective-permute-start(f32[3,8,1,128]{3,2,1,0:T(1,128)S(1)} %get-tuple-element.611), channel_id=1, source_target_pairs={{0,64},{64,128},{128,192},{192,256},{256,320},{320,384},{384,448},... | collective-permute-start | bytes 36872 | tf_op jit(solution)/shard_map/ppermute | solution.py:75
  3.3 13.1 %collective-permute-start = (f32[3,8,1,128]{3,2,1,0:T(1,128)S(1)}, f32[3,8,1,128]{3,2,1,0:T(1,128)S(1)}, u32[]{:S(2)}, u32[]{:S(2)}) collective-permute-start(f32[3,8,1,128]{3,2,1,0:T(1,128)S(1)} %get-tuple-element.612), channel_id=1, source_target_pairs={{64,0},{128,64},{192,128},{256,192},{320,256},{384,320},{448,384},... | collective-permute-start | bytes 36872 | tf_op jit(solution)/shard_map/ppermute | solution.py:76
  7.4 10.1 %collective-permute-start.2 = (f32[3,1,32,128]{3,2,1,0:T(8,128)S(1)}, f32[3,1,32,128]{3,2,1,0:T(8,128)S(1)}, u32[]{:S(2)}, u32[]{:S(2)}) collective-permute-start(f32[3,1,32,128]{3,2,1,0:T(8,128)S(1)} %get-tuple-element.609), channel_id=1, source_target_pairs={{1,0},{2,1},{3,2},{4,3},{5,4},{6,5},{7,6},{8,7},{9,8},{10,9},{11,1... | collective-permute-start | bytes 147464 | tf_op jit(solution)/shard_map/ppermute | solution.py:76
  10.5 5.9 %collective-permute-start.3 = (f32[3,1,32,128]{3,2,1,0:T(8,128)S(1)}, f32[3,1,32,128]{3,2,1,0:T(8,128)S(1)}, u32[]{:S(2)}, u32[]{:S(2)}) collective-permute-start(f32[3,1,32,128]{3,2,1,0:T(8,128)S(1)} %get-tuple-element.610), channel_id=1, source_target_pairs={{0,1},{1,2},{2,3},{3,4},{4,5},{5,6},{6,7},{7,8},{8,9},{9,10},{10,1... | collective-permute-start | bytes 147464 | tf_op jit(solution)/shard_map/ppermute | solution.py:75
  14.1 64.0 %copy-start.10 = (s32[128]{0:T(128)}, s32[128]{0:T(128)S(1)}, u32[]{:S(2)}) copy-start(s32[128]{0:T(128)S(1)} %and_select_fusion.6) | copy-start | bytes 1540
  14.1 113.0 %copy-start.12 = (s32[64]{0:T(128)}, s32[64]{0:T(128)S(1)}, u32[]{:S(2)}) copy-start(s32[64]{0:T(128)S(1)} %and_select_fusion.4) | copy-start | bytes 772
  14.7 112.7 %copy-start.49 = (s32[8]{0:T(128)}, s32[8]{0:T(128)S(1)}, u32[]{:S(2)}) copy-start(s32[8]{0:T(128)S(1)} %broadcast_add_fusion.2) | copy-start | bytes 100
  16.3 0.9 copy-start.3
  17.3 0.9 copy-start
  23.7 25.3 %all-to-all-start = ((f32[64,1,384]{2,1,0:T(1,128)}), f32[64,1,384]{2,1,0:T(1,128)S(1)}, u32[]{:S(2)}, u32[]{:S(2)}) async-start(f32[64,1,384]{2,1,0:T(1,128)} %reshape.2544), calls=%async_computation | async-start | bytes 196608 | tf_op jit(solution)/shard_map/all_to_all | solution.py:270
  55.6 13.9 %all-to-all-start.1 = ((f32[64,1,128]{2,1,0:T(1,128)}), f32[64,1,128]{2,1,0:T(1,128)S(1)}, u32[]{:S(2)}, u32[]{:S(2)}) async-start(f32[64,1,128]{2,1,0:T(1,128)} %reshape.2546), calls=%async_computation.1 | async-start | bytes 65536 | tf_op jit(solution)/shard_map/all_to_all | solution.py:274
  70.6 4.4 collective-permute-start.4
  73.6 4.4 collective-permute-start.5
  79.9 18.6 %all-to-all-start.2 = ((f32[64,6,1,16]{3,2,1,0:T(1,128)}), f32[64,6,1,16]{3,2,1,0:T(1,128)S(1)}, u32[]{:S(2)}, u32[]{:S(2)}) async-start(f32[64,6,1,16]{3,2,1,0:T(1,128)} %copy.294), calls=%async_computation.2 | async-start | bytes 393216 | tf_op jit(solution)/shard_map/all_to_all | solution.py:270
  103.9 14.6 %all-to-all-start.3 = ((f32[2,64,16]{2,0,1:T(2,128)}), f32[2,64,16]{2,0,1:T(2,128)S(1)}, u32[]{:S(2)}, u32[]{:S(2)}) async-start(f32[2,64,16]{2,0,1:T(2,128)} %copy.300), calls=%async_computation.3 | async-start | bytes 131072 | tf_op jit(solution)/shard_map/all_to_all | solution.py:274
  118.9 4.9 collective-permute-start.6
  122.4 4.6 collective-permute-start.7
  128.3 4.3 collective-permute-start.8
  138.1 19.8 %all-to-all-start.4 = ((f32[64,6,1,256]{3,2,1,0:T(1,128)}), f32[64,6,1,256]{3,2,1,0:T(1,128)S(1)}, u32[]{:S(2)}, u32[]{:S(2)}) async-start(f32[64,6,1,256]{3,2,1,0:T(1,128)} %broadcast_in_dim.45), calls=%async_computation.4 | async-start | bytes 786432 | tf_op jit(solution)/shard_map/all_to_all | solution.py:42
  164.6 0.7 copy-start.22
  164.8 0.7 copy-start.4
  165.6 5.0 collective-permute-start.9
  169.2 4.3 collective-permute-start.10
  174.3 0.7 copy-start.25
  174.3 0.7 copy-start.46
  175.0 0.7 copy-start.24
  175.0 0.7 copy-start.51
  175.7 0.7 copy-start.7
  176.4 0.7 copy-start.9
  177.1 0.7 copy-start.23
  177.8 0.7 copy-start.8
  178.6 4.6 collective-permute-start.11
  188.5 18.6 %all-to-all-start.5 = ((f32[64,1,384]{2,1,0:T(1,128)}), f32[64,1,384]{2,1,0:T(1,128)S(1)}, u32[]{:S(2)}, u32[]{:S(2)}) async-start(f32[64,1,384]{2,1,0:T(1,128)} %reshape.2548), calls=%async_computation.5 | async-start | bytes 196608 | tf_op jit(solution)/shard_map/all_to_all | solution.py:42
  211.2 4.5 collective-permute-start.12
  214.4 4.3 collective-permute-start.13
  221.0 0.7 copy-start.39
  222.0 6.0 %collective-permute-start.14 = (f32[7,2,2,8]{3,2,1,0:T(2,128)S(1)}, f32[7,2,2,8]{3,2,1,0:T(2,128)S(1)}, u32[]{:S(2)}, u32[]{:S(2)}) collective-permute-start(f32[7,2,2,8]{3,2,1,0:T(2,128)S(1)} %fusion.40), channel_id=1, source_target_pairs={{0,4},{1,5},{2,6},{3,7},{4,0},{5,1},{6,2},{7,3},{8,12},{9,13},{10,... | collective-permute-start | bytes 2696 | tf_op jit(solution)/shard_map/ppermute | solution.py:88
  235.5 19.3 %all-to-all-start.6 = ((f32[64,6,1,16]{3,2,1,0:T(1,128)}), f32[64,6,1,16]{3,2,1,0:T(1,128)S(1)}, u32[]{:S(2)}, u32[]{:S(2)}) async-start(f32[64,6,1,16]{3,2,1,0:T(1,128)} %broadcast_in_dim.49), calls=%async_computation.6 | async-start | bytes 393216 | tf_op jit(solution)/shard_map/all_to_all | solution.py:42
  257.8 4.2 collective-permute-start.15
  260.7 4.3 collective-permute-start.16
  269.3 4.4 collective-permute-start.17
  274.7 18.4 %all-to-all-start.7 = ((f32[64,6,1,4]{1,3,2,0:T(4,128)}), f32[64,6,1,4]{1,3,2,0:T(4,128)S(1)}, u32[]{:S(2)}, u32[]{:S(2)}) async-start(f32[64,6,1,4]{1,3,2,0:T(4,128)} %broadcast_in_dim.51), calls=%async_computation.7 | async-start | bytes 262144 | tf_op jit(solution)/shard_map/all_to_all | solution.py:42
  295.5 5.3 %collective-permute-start.19 = (f32[4,1,4]{2,0,1:T(4,128)S(1)}, f32[4,1,4]{2,0,1:T(4,128)S(1)}, u32[]{:S(2)}, u32[]{:S(2)}) collective-permute-start(f32[4,1,4]{2,0,1:T(4,128)S(1)} %fusion.450), channel_id=1, source_target_pairs={{0,64},{64,128},{128,192},{192,256},{256,320},{320,384},{384,448},... | collective-permute-start | bytes 200 | tf_op jit(solution)/shard_map/ppermute | solution.py:58
  296.8 4.7 collective-permute-start.18
  302.4 16.9 %all-to-all-start.8 = ((f32[64,6,1,4]{1,3,2,0:T(4,128)}), f32[64,6,1,4]{1,3,2,0:T(4,128)S(1)}, u32[]{:S(2)}, u32[]{:S(2)}) async-start(f32[64,6,1,4]{1,3,2,0:T(4,128)} %broadcast_in_dim.53), calls=%async_computation.8 | async-start | bytes 262144 | tf_op jit(solution)/shard_map/all_to_all | solution.py:42
  321.9 5.3 %collective-permute-start.20 = (f32[4,1,8]{2,1,0:T(1,128)S(1)}, f32[4,1,8]{2,1,0:T(1,128)S(1)}, u32[]{:S(2)}, u32[]{:S(2)}) collective-permute-start(f32[4,1,8]{2,1,0:T(1,128)S(1)} %get-tuple-element.1200), channel_id=1, source_target_pairs={{64,0},{128,64},{192,128},{256,192},{320,256},{384,320},{448,384},... | collective-permute-start | bytes 392 | tf_op jit(solution)/shard_map/ppermute | solution.py:60
  325.9 4.3 collective-permute-start.21
  331.3 18.5 %all-to-all-start.9 = ((f32[64,6,1,16]{3,2,1,0:T(1,128)}), f32[64,6,1,16]{3,2,1,0:T(1,128)S(1)}, u32[]{:S(2)}, u32[]{:S(2)}) async-start(f32[64,6,1,16]{3,2,1,0:T(1,128)} %broadcast_in_dim.57), calls=%async_computation.9 | async-start | bytes 393216 | tf_op jit(solution)/shard_map/all_to_all | solution.py:42
  352.5 4.2 collective-permute-start.22
  355.4 5.5 %collective-permute-start.23 = (f32[4,1,16]{2,1,0:T(1,128)S(1)}, f32[4,1,16]{2,1,0:T(1,128)S(1)}, u32[]{:S(2)}, u32[]{:S(2)}) collective-permute-start(f32[4,1,16]{2,1,0:T(1,128)S(1)} %get-tuple-element.1077), channel_id=1, source_target_pairs={{0,64},{64,128},{128,192},{192,256},{256,320},{320,384},{384,448},... | collective-permute-start | bytes 776 | tf_op jit(solution)/shard_map/ppermute | solution.py:58
  363.1 16.3 %all-to-all-start.10 = ((f32[64,1,384]{2,1,0:T(1,128)}), f32[64,1,384]{2,1,0:T(1,128)S(1)}, u32[]{:S(2)}, u32[]{:S(2)}) async-start(f32[64,1,384]{2,1,0:T(1,128)} %reshape.2550), calls=%async_computation.10 | async-start | bytes 196608 | tf_op jit(solution)/shard_map/all_to_all | solution.py:42
  383.9 6.2 %collective-permute-start.24 = (f32[4,1,32]{2,1,0:T(1,128)S(1)}, f32[4,1,32]{2,1,0:T(1,128)S(1)}, u32[]{:S(2)}, u32[]{:S(2)}) collective-permute-start(f32[4,1,32]{2,1,0:T(1,128)S(1)} %get-tuple-element.953), channel_id=1, source_target_pairs={{64,0},{128,64},{192,128},{256,192},{320,256},{384,320},{448,384},... | collective-permute-start | bytes 1544 | tf_op jit(solution)/shard_map/ppermute | solution.py:60
  388.7 4.6 collective-permute-start.25
  394.1 0.7 copy-start.14
  395.8 20.9 %all-to-all-start.11 = ((f32[64,6,1,256]{3,2,1,0:T(1,128)}), f32[64,6,1,256]{3,2,1,0:T(1,128)S(1)}, u32[]{:S(2)}, u32[]{:S(2)}) async-start(f32[64,6,1,256]{3,2,1,0:T(1,128)} %broadcast_in_dim.63), calls=%async_computation.11 | async-start | bytes 786432 | tf_op jit(solution)/shard_map/all_to_all | solution.py:42
  421.8 0.7 copy-start.16
  423.5 5.0 collective-permute-start.26
  427.1 4.3 collective-permute-start.27
  471.2 4.3 collective-permute-start.28
  474.1 4.4 collective-permute-start.29
  480.8 16.6 %all-to-all-start.14 = ((f32[64,1,384]{2,1,0:T(1,128)}), f32[64,1,384]{2,1,0:T(1,128)S(1)}, u32[]{:S(2)}, u32[]{:S(2)}) async-start(f32[64,1,384]{2,1,0:T(1,128)} %reshape.2552), calls=%async_computation.14 | async-start | bytes 196608 | tf_op jit(solution)/shard_map/all_to_all | solution.py:270
  503.9 13.9 %all-to-all-start.15 = ((f32[64,1,128]{2,1,0:T(1,128)}), f32[64,1,128]{2,1,0:T(1,128)S(1)}, u32[]{:S(2)}, u32[]{:S(2)}) async-start(f32[64,1,128]{2,1,0:T(1,128)} %reshape.2554), calls=%async_computation.15 | async-start | bytes 65536 | tf_op jit(solution)/shard_map/all_to_all | solution.py:274
  (33 other events, 21.7 us)

commit v4 on v2

--- a/solution.py
+++ b/solution.py
@@ -264,9 +264,10 @@
     shape = head.shape
     packed = jnp.stack(
         [level["alpha"], level["beta"], level["gamma"], level["delta"], head, tail]
-    ).reshape(6, 1, -1)
+    ).reshape(6, -1)
     if group == 1:
-        moved = exchange_by_chip(packed, (("gy_0", "gy_1"), "gy_2"), (1, 0), 2, 1)
+        parts = in_blocks(packed, 1, lax.axis_size(GY))
+        moved = jnp.moveaxis(turned_blocks(parts, (("gy_0", "gy_1"), "gy_2"), (1, 0)), 0, 1)
         prev_last, next_first = reduced_local(
             moved[0], moved[1], moved[2], moved[3], moved[4], moved[5]
         )
@@ -274,7 +275,7 @@
             jnp.stack([prev_last, next_first]), GY, split_axis=1, concat_axis=2, tiled=True
         )
         return (back[0, 0].reshape(shape), back[1, 0].reshape(shape))
-    whole = gather_directly(packed, GY, 1)
+    whole = jnp.moveaxis(copy_for_each(packed, GY), 0, 1)
     whole = whole.reshape(6, whole.shape[1] // group, group, -1)[:, :, 0]
     prev_last, next_first = reduced_local(
         whole[0], whole[1], whole[2], whole[3], whole[4], whole[5]

time: 517 us -> 584 us (1.13)
  the two profiles are of different devices: /device:TPU:57 before, /device:TPU:1 now
where the time goes in v4:
time: 584 us; the launch traced here: 573 us
  waiting for transfers between devices  192 us (33%)
  starting transfers between devices  165 us (28%)
  local copies, waits for them, and re-layouts  108 us (18%)
  blocking collectives  48.1 us (8%)
  other arithmetic  35 us (6%)
  matrix products  15.6 us (3%)
  between operations  9.57 us (2%)
    all_to_all x8, waiting for transfers between devices, copy_for_each(): lax.all_to_all(jnp.broadcast_to(x[None], (count, *x.shape)), axis, 0, 0,...  99.4 us
    all_to_all x8, starting transfers between devices, copy_for_each(): lax.all_to_all(jnp.broadcast_to(x[None], (count, *x.shape)), axis, 0, 0,...  51 us
    slice x940, local copies, waits for them, and re-layouts, reduced_local(): inclusive = lax.associative_scan(chain_forward, terms, axis=0)  44.7 us
    unnamed x335, local copies, waits for them, and re-layouts  39 us
    ppermute x11, starting transfers between devices, padded(): lax.ppermute(tail, axis, [(i, (i + 1) % count) for i in range(ends)])  35.2 us
    ppermute x11, waiting for transfers between devices, padded(): lax.ppermute(head, axis, [((i + 1) % count, i) for i in range(ends)])  33 us
    all_to_all x5, blocking collectives, turned_blocks(): lax.all_to_all(parts, axes[k], split_axis=k, concat_axis=k, tiled=True)  33 us
    all_to_all x3, waiting for transfers between devices, reduced_moved(): lax.all_to_all(jnp.stack([prev_last, next_first]), GY, split_axis=1, conc...  28.8 us
  transfers between devices with their start and end apart: 44, of which 29 were waited for; matrix products, arithmetic and copies ran while one was open for 2% of the time, Pallas kernels for 0%

profile of v4, /device:TPU:1, one launch (start us, length us, event | category | flops | bytes accessed | tf_op | source)
XLA Modules:
  0.0 573.3 jit_solution(10871803784985867823)
XLA Ops:
  3.3 4.6 collective-permute-start.1
  8.0 4.4 collective-permute-start.3
  12.4 5.5 collective-permute-start.2
  24.2 3.5 all_to_all.116
  30.3 10.7 %all-to-all-start.1 = ((f32[32,1,768]{2,1,0:T(1,128)}), f32[32,1,768]{2,1,0:T(1,128)S(1)}, u32[]{:S(2)}, u32[]{:S(2)}) async-start(f32[32,1,768]{2,1,0:T(1,128)} %reshape.2542), calls=%async_computation.1 | async-start | bytes 196608 | tf_op jit(solution)/shard_map/all_to_all | solution.py:30
  43.1 7.0 %all-to-all-done.1 = f32[32,1,768]{2,1,0:T(1,128)S(1)} async-done(((f32[32,1,768]{2,1,0:T(1,128)}), f32[32,1,768]{2,1,0:T(1,128)S(1)}, u32[]{:S(2)}, u32[]{:S(2)}) %all-to-all-start.1) | async-done | bytes 98336 | tf_op jit(solution)/shard_map/all_to_all | solution.py:30
  56.7 5.8 %all-to-all-start.2 = ((f32[64,1,128]{2,1,0:T(1,128)}), f32[64,1,128]{2,1,0:T(1,128)S(1)}, u32[]{:S(2)}, u32[]{:S(2)}) async-start(f32[64,1,128]{2,1,0:T(1,128)} %reshape.2544), calls=%async_computation.2 | async-start | bytes 65536 | tf_op jit(solution)/shard_map/all_to_all | solution.py:274
  62.5 9.4 %all-to-all-done.2 = f32[64,1,128]{2,1,0:T(1,128)S(1)} async-done(((f32[64,1,128]{2,1,0:T(1,128)}), f32[64,1,128]{2,1,0:T(1,128)S(1)}, u32[]{:S(2)}, u32[]{:S(2)}) %all-to-all-start.2) | async-done | bytes 32800 | tf_op jit(solution)/shard_map/all_to_all | solution.py:274
  73.2 3.2 collective-permute-start.5
  77.8 2.9 collective-permute-done.4
  82.5 5.5 all_to_all.117
  89.8 4.3 all-to-all-start.4
  94.3 8.5 %all-to-all-done.4 = f32[32,1,192]{2,1,0:T(1,128)S(1)} async-done(((f32[32,1,192]{2,1,0:T(1,128)}), f32[32,1,192]{2,1,0:T(1,128)S(1)}, u32[]{:S(2)}, u32[]{:S(2)}) %all-to-all-start.4) | async-done | bytes 24608 | tf_op jit(solution)/shard_map/all_to_all | solution.py:30
  109.2 5.5 all-to-all-start.5
  114.9 9.9 %all-to-all-done.5 = f32[2,64,16]{2,0,1:T(2,128)S(1)} async-done(((f32[2,64,16]{2,0,1:T(2,128)}), f32[2,64,16]{2,0,1:T(2,128)S(1)}, u32[]{:S(2)}, u32[]{:S(2)}) %all-to-all-start.5) | async-done | bytes 8224 | tf_op jit(solution)/shard_map/all_to_all | solution.py:274
  125.2 4.0 collective-permute-start.7
  130.6 3.2 collective-permute-done.6
  135.1 3.5 collective-permute-start.8
  144.6 4.4 all-to-all-start.6
  152.0 14.8 %all-to-all-done.6 = f32[64,6,256]{2,1,0:T(8,128)S(1)} async-done(((f32[64,6,256]{2,1,0:T(8,128)}), f32[64,6,256]{2,1,0:T(8,128)S(1)}, u32[]{:S(2)}, u32[]{:S(2)}) %all-to-all-start.6) | async-done | bytes 393248 | tf_op jit(solution)/shard_map/all_to_all | solution.py:42
  208.6 4.4 collective-permute-start.10
  214.4 3.2 collective-permute-done.9
  222.7 3.0 collective-permute-start.11
  229.9 8.0 %all-to-all-start.7 = ((f32[64,1,384]{2,1,0:T(1,128)}), f32[64,1,384]{2,1,0:T(1,128)S(1)}, u32[]{:S(2)}, u32[]{:S(2)}) async-start(f32[64,1,384]{2,1,0:T(1,128)} %reshape.2550), calls=%async_computation.7 | async-start | bytes 196608 | tf_op jit(solution)/shard_map/all_to_all | solution.py:42
  238.3 10.2 %all-to-all-done.7 = f32[64,1,384]{2,1,0:T(1,128)S(1)} async-done(((f32[64,1,384]{2,1,0:T(1,128)}), f32[64,1,384]{2,1,0:T(1,128)S(1)}, u32[]{:S(2)}, u32[]{:S(2)}) %all-to-all-start.7) | async-done | bytes 98336 | tf_op jit(solution)/shard_map/all_to_all | solution.py:42
  252.6 3.6 collective-permute-start.13
  257.6 3.0 collective-permute-done.12
  262.8 3.0 collective-permute-start.14
  265.9 2.9 collective-permute-done.14
  270.7 7.0 %all-to-all-start.8 = ((f32[64,6,16]{2,1,0:T(8,128)}), f32[64,6,16]{2,1,0:T(8,128)S(1)}, u32[]{:S(2)}, u32[]{:S(2)}) async-start(f32[64,6,16]{2,1,0:T(8,128)} %broadcast_in_dim.49), calls=%async_computation.8 | async-start | bytes 524288 | tf_op jit(solution)/shard_map/all_to_all | solution.py:42
  279.0 11.9 %all-to-all-done.8 = f32[64,6,16]{2,1,0:T(8,128)S(1)} async-done(((f32[64,6,16]{2,1,0:T(8,128)}), f32[64,6,16]{2,1,0:T(8,128)S(1)}, u32[]{:S(2)}, u32[]{:S(2)}) %all-to-all-start.8) | async-done | bytes 24608 | tf_op jit(solution)/shard_map/all_to_all | solution.py:42
  293.3 2.9 collective-permute-start.16
  297.5 3.0 collective-permute-done.15
  300.9 2.9 collective-permute-start.17
  306.3 7.4 %all-to-all-start.9 = ((f32[64,6,4]{1,2,0:T(4,128)}), f32[64,6,4]{1,2,0:T(4,128)S(1)}, u32[]{:S(2)}, u32[]{:S(2)}) async-start(f32[64,6,4]{1,2,0:T(4,128)} %broadcast_in_dim.51), calls=%async_computation.9 | async-start | bytes 262144 | tf_op jit(solution)/shard_map/all_to_all | solution.py:42
  313.7 11.1 %all-to-all-done.9 = f32[64,6,4]{1,2,0:T(4,128)S(1)} async-done(((f32[64,6,4]{1,2,0:T(4,128)}), f32[64,6,4]{1,2,0:T(4,128)S(1)}, u32[]{:S(2)}, u32[]{:S(2)}) %all-to-all-start.9) | async-done | bytes 6176 | tf_op jit(solution)/shard_map/all_to_all | solution.py:42
  327.2 2.9 collective-permute-start.19
  331.4 3.0 collective-permute-done.18
  335.3 5.9 %all-to-all-start.10 = ((f32[64,6,4]{1,2,0:T(4,128)}), f32[64,6,4]{1,2,0:T(4,128)S(1)}, u32[]{:S(2)}, u32[]{:S(2)}) async-start(f32[64,6,4]{1,2,0:T(4,128)} %broadcast_in_dim.53), calls=%async_computation.10 | async-start | bytes 262144 | tf_op jit(solution)/shard_map/all_to_all | solution.py:42
  341.2 11.3 %all-to-all-done.10 = f32[64,6,4]{1,2,0:T(4,128)S(1)} async-done(((f32[64,6,4]{1,2,0:T(4,128)}), f32[64,6,4]{1,2,0:T(4,128)S(1)}, u32[]{:S(2)}, u32[]{:S(2)}) %all-to-all-start.10) | async-done | bytes 6176 | tf_op jit(solution)/shard_map/all_to_all | solution.py:42
  355.1 2.9 collective-permute-start.21
  359.3 3.0 collective-permute-done.20
  363.3 6.2 %all-to-all-start.11 = ((f32[64,6,16]{2,1,0:T(8,128)}), f32[64,6,16]{2,1,0:T(8,128)S(1)}, u32[]{:S(2)}, u32[]{:S(2)}) async-start(f32[64,6,16]{2,1,0:T(8,128)} %broadcast_in_dim.57), calls=%async_computation.11 | async-start | bytes 524288 | tf_op jit(solution)/shard_map/all_to_all | solution.py:42
  369.5 13.0 %all-to-all-done.11 = f32[64,6,16]{2,1,0:T(8,128)S(1)} async-done(((f32[64,6,16]{2,1,0:T(8,128)}), f32[64,6,16]{2,1,0:T(8,128)S(1)}, u32[]{:S(2)}, u32[]{:S(2)}) %all-to-all-start.11) | async-done | bytes 24608 | tf_op jit(solution)/shard_map/all_to_all | solution.py:42
  385.2 2.9 collective-permute-start.23
  389.4 3.0 collective-permute-done.22
  393.5 6.3 %all-to-all-start.12 = ((f32[64,1,384]{2,1,0:T(1,128)}), f32[64,1,384]{2,1,0:T(1,128)S(1)}, u32[]{:S(2)}, u32[]{:S(2)}) async-start(f32[64,1,384]{2,1,0:T(1,128)} %reshape.2552), calls=%async_computation.12 | async-start | bytes 196608 | tf_op jit(solution)/shard_map/all_to_all | solution.py:42
  399.8 10.6 %all-to-all-done.12 = f32[64,1,384]{2,1,0:T(1,128)S(1)} async-done(((f32[64,1,384]{2,1,0:T(1,128)}), f32[64,1,384]{2,1,0:T(1,128)S(1)}, u32[]{:S(2)}, u32[]{:S(2)}) %all-to-all-start.12) | async-done | bytes 98336 | tf_op jit(solution)/shard_map/all_to_all | solution.py:42
  414.8 2.9 collective-permute-start.25
  419.1 3.0 collective-permute-done.24
  425.0 5.9 %all-to-all-start.13 = ((f32[64,6,256]{2,1,0:T(8,128)}), f32[64,6,256]{2,1,0:T(8,128)S(1)}, u32[]{:S(2)}, u32[]{:S(2)}) async-start(f32[64,6,256]{2,1,0:T(8,128)} %broadcast_in_dim.63), calls=%async_computation.13 | async-start | bytes 1048576 | tf_op jit(solution)/shard_map/all_to_all | solution.py:42
  432.2 16.5 %all-to-all-done.13 = f32[64,6,256]{2,1,0:T(8,128)S(1)} async-done(((f32[64,6,256]{2,1,0:T(8,128)}), f32[64,6,256]{2,1,0:T(8,128)S(1)}, u32[]{:S(2)}, u32[]{:S(2)}) %all-to-all-start.13) | async-done | bytes 393248 | tf_op jit(solution)/shard_map/all_to_all | solution.py:42
  470.5 2.9 collective-permute-start.27
  474.7 3.0 collective-permute-done.26
  478.5 5.2 all_to_all.118
  484.9 13.6 %all_to_all.119 = f32[32,1,192]{2,1,0:T(1,128)S(1)} all-to-all(f32[32,1,192]{2,1,0:T(1,128)S(1)} %reshape.2556), channel_id=1, replica_groups=mesh['gx'=8,'gy_0'=8,'gy_1'=4,'gy_2'=2] {'gy_0','gy_1'}, dimensions={0} | all-to-all | bytes 49152 | tf_op jit(solution)/shard_map/all_to_all | solution.py:30
  504.3 15.1 %all_to_all.120 = f32[2,64,16]{2,0,1:T(2,128)S(1)} all-to-all(f32[2,64,16]{2,0,1:T(2,128)S(1)} %copy.316), channel_id=1, replica_groups=mesh['gx'=8,'gy_0'=8,'gy_1'=4,'gy_2'=2] {'gy_0','gy_1','gy_2'}, dimensions={1} | all-to-all | bytes 16384 | tf_op jit(solution)/shard_map/all_to_all | solution.py:274
  520.9 2.8 collective-permute-start.29
  525.2 2.9 collective-permute-done.28
  528.8 5.3 all_to_all.121
  536.1 3.9 all-to-all-start.18
  540.0 9.1 %all-to-all-done.18 = f32[32,1,768]{2,1,0:T(1,128)S(1)} async-done(((f32[32,1,768]{2,1,0:T(1,128)}), f32[32,1,768]{2,1,0:T(1,128)S(1)}, u32[]{:S(2)}, u32[]{:S(2)}) %all-to-all-start.18) | async-done | bytes 98336 | tf_op jit(solution)/shard_map/all_to_all | solution.py:30
  555.7 5.8 %all-to-all-start.19 = ((f32[64,1,128]{2,1,0:T(1,128)}), f32[64,1,128]{2,1,0:T(1,128)S(1)}, u32[]{:S(2)}, u32[]{:S(2)}) async-start(f32[64,1,128]{2,1,0:T(1,128)} %reshape.2562), calls=%async_computation.19 | async-start | bytes 65536 | tf_op jit(solution)/shard_map/all_to_all | solution.py:274
  561.5 9.4 %all-to-all-done.19 = f32[64,1,128]{2,1,0:T(1,128)S(1)} async-done(((f32[64,1,128]{2,1,0:T(1,128)}), f32[64,1,128]{2,1,0:T(1,128)S(1)}, u32[]{:S(2)}, u32[]{:S(2)}) %all-to-all-start.19) | async-done | bytes 32800 | tf_op jit(solution)/shard_map/all_to_all | solution.py:274
  (2998 shorter events, 177.8 us)
Async XLA Ops:
  1.0 0.9 copy-start.1
  1.0 1.0 copy-start.2
  2.0 18.9 %collective-permute-start = (f32[3,8,1,128]{3,2,1,0:T(1,128)S(1)}, f32[3,8,1,128]{3,2,1,0:T(1,128)S(1)}, u32[]{:S(2)}, u32[]{:S(2)}) collective-permute-start(f32[3,8,1,128]{3,2,1,0:T(1,128)S(1)} %get-tuple-element.612), channel_id=1, source_target_pairs={{64,0},{128,64},{192,128},{256,192},{320,256},{384,320},{448,384},... | collective-permute-start | bytes 36872 | tf_op jit(solution)/shard_map/ppermute | solution.py:76
  3.3 17.6 %collective-permute-start.1 = (f32[3,8,1,128]{3,2,1,0:T(1,128)S(1)}, f32[3,8,1,128]{3,2,1,0:T(1,128)S(1)}, u32[]{:S(2)}, u32[]{:S(2)}) collective-permute-start(f32[3,8,1,128]{3,2,1,0:T(1,128)S(1)} %get-tuple-element.611), channel_id=1, source_target_pairs={{0,64},{64,128},{128,192},{192,256},{256,320},{320,384},{384,448},... | collective-permute-start | bytes 36872 | tf_op jit(solution)/shard_map/ppermute | solution.py:75
  8.0 12.9 %collective-permute-start.3 = (f32[3,1,32,128]{3,2,1,0:T(8,128)S(1)}, f32[3,1,32,128]{3,2,1,0:T(8,128)S(1)}, u32[]{:S(2)}, u32[]{:S(2)}) collective-permute-start(f32[3,1,32,128]{3,2,1,0:T(8,128)S(1)} %get-tuple-element.610), channel_id=1, source_target_pairs={{0,1},{1,2},{2,3},{3,4},{4,5},{5,6},{6,7},{7,8},{8,9},{9,10},{10,1... | collective-permute-start | bytes 147464 | tf_op jit(solution)/shard_map/ppermute | solution.py:75
  12.4 9.5 %collective-permute-start.2 = (f32[3,1,32,128]{3,2,1,0:T(8,128)S(1)}, f32[3,1,32,128]{3,2,1,0:T(8,128)S(1)}, u32[]{:S(2)}, u32[]{:S(2)}) collective-permute-start(f32[3,1,32,128]{3,2,1,0:T(8,128)S(1)} %get-tuple-element.609), channel_id=1, source_target_pairs={{1,0},{2,1},{3,2},{4,3},{5,4},{6,5},{7,6},{8,7},{9,8},{10,9},{11,1... | collective-permute-start | bytes 147464 | tf_op jit(solution)/shard_map/ppermute | solution.py:76
  18.0 62.9 %copy-start.38 = (s32[128]{0:T(128)}, s32[128]{0:T(128)S(1)}, u32[]{:S(2)}) copy-start(s32[128]{0:T(128)S(1)} %and_select_fusion.6) | copy-start | bytes 1540
  18.0 115.9 %copy-start.40 = (s32[64]{0:T(128)}, s32[64]{0:T(128)S(1)}, u32[]{:S(2)}) copy-start(s32[64]{0:T(128)S(1)} %and_select_fusion.4) | copy-start | bytes 772
  18.1 116.1 %copy-start.109 = (s32[8]{0:T(128)}, s32[8]{0:T(128)S(1)}, u32[]{:S(2)}) copy-start(s32[8]{0:T(128)S(1)} %broadcast_add_fusion.2) | copy-start | bytes 100
  20.8 0.9 copy-start.3
  21.8 0.9 copy-start
  30.3 19.8 %all-to-all-start.1 = ((f32[32,1,768]{2,1,0:T(1,128)}), f32[32,1,768]{2,1,0:T(1,128)S(1)}, u32[]{:S(2)}, u32[]{:S(2)}) async-start(f32[32,1,768]{2,1,0:T(1,128)} %reshape.2542), calls=%async_computation.1 | async-start | bytes 196608 | tf_op jit(solution)/shard_map/all_to_all | solution.py:30
  56.7 15.2 %all-to-all-start.2 = ((f32[64,1,128]{2,1,0:T(1,128)}), f32[64,1,128]{2,1,0:T(1,128)S(1)}, u32[]{:S(2)}, u32[]{:S(2)}) async-start(f32[64,1,128]{2,1,0:T(1,128)} %reshape.2544), calls=%async_computation.2 | async-start | bytes 65536 | tf_op jit(solution)/shard_map/all_to_all | solution.py:274
  73.2 4.6 collective-permute-start.5
  76.4 4.4 collective-permute-start.4
  89.8 13.0 %all-to-all-start.4 = ((f32[32,1,192]{2,1,0:T(1,128)}), f32[32,1,192]{2,1,0:T(1,128)S(1)}, u32[]{:S(2)}, u32[]{:S(2)}) async-start(f32[32,1,192]{2,1,0:T(1,128)} %reshape.2548), calls=%async_computation.4 | async-start | bytes 65536 | tf_op jit(solution)/shard_map/all_to_all | solution.py:30
  109.2 15.6 %all-to-all-start.5 = ((f32[2,64,16]{2,0,1:T(2,128)}), f32[2,64,16]{2,0,1:T(2,128)S(1)}, u32[]{:S(2)}, u32[]{:S(2)}) async-start(f32[2,64,16]{2,0,1:T(2,128)} %copy.245), calls=%async_computation.5 | async-start | bytes 131072 | tf_op jit(solution)/shard_map/all_to_all | solution.py:274
  125.2 5.4 collective-permute-start.7
  129.2 4.6 collective-permute-start.6
  135.1 4.3 collective-permute-start.8
  141.0 1.3 copy-start.4
  141.0 66.2 %copy-start.6 = (f32[1,8,32]{2,1,0:T(8,128)}, f32[1,8,32]{2,1,0:T(8,128)S(1)}, u32[]{:S(2)}) copy-start(f32[1,8,32]{2,1,0:T(8,128)S(1)} %get-tuple-element.442) | copy-start | bytes 3076
  142.3 1.4 copy-start.69
  144.6 22.2 %all-to-all-start.6 = ((f32[64,6,256]{2,1,0:T(8,128)}), f32[64,6,256]{2,1,0:T(8,128)S(1)}, u32[]{:S(2)}, u32[]{:S(2)}) async-start(f32[64,6,256]{2,1,0:T(8,128)} %broadcast_in_dim.45), calls=%async_computation.6 | async-start | bytes 1048576 | tf_op jit(solution)/shard_map/all_to_all | solution.py:42
  176.7 0.7 copy-start.28
  176.7 0.8 copy-start.29
  176.7 0.8 copy-start.33
  184.7 7.4 %copy-start.60 = (f32[2,256]{1,0:T(2,128)}, f32[2,256]{1,0:T(2,128)S(1)}, u32[]{:S(2)}) copy-start(f32[2,256]{1,0:T(2,128)S(1)} %slice.8449) | copy-start | bytes 6148
  184.8 7.4 %copy-start.62 = (f32[2,256]{1,0:T(2,128)}, f32[2,256]{1,0:T(2,128)S(1)}, u32[]{:S(2)}) copy-start(f32[2,256]{1,0:T(2,128)S(1)} %slice.8437) | copy-start | bytes 6148
  184.8 1.2 copy-start.43
  187.2 1.2 copy-start.44
  204.6 0.7 copy-start.10
  208.6 5.8 %collective-permute-start.10 = (f32[4,1,32]{2,1,0:T(1,128)S(1)}, f32[4,1,32]{2,1,0:T(1,128)S(1)}, u32[]{:S(2)}, u32[]{:S(2)}) collective-permute-start(f32[4,1,32]{2,1,0:T(1,128)S(1)} %get-tuple-element.964), channel_id=1, source_target_pairs={{0,64},{64,128},{128,192},{192,256},{256,320},{320,384},{384,448},... | collective-permute-start | bytes 1544 | tf_op jit(solution)/shard_map/ppermute | solution.py:58
  213.0 4.6 collective-permute-start.9
  222.7 4.6 collective-permute-start.11
  229.9 18.6 %all-to-all-start.7 = ((f32[64,1,384]{2,1,0:T(1,128)}), f32[64,1,384]{2,1,0:T(1,128)S(1)}, u32[]{:S(2)}, u32[]{:S(2)}) async-start(f32[64,1,384]{2,1,0:T(1,128)} %reshape.2550), calls=%async_computation.7 | async-start | bytes 196608 | tf_op jit(solution)/shard_map/all_to_all | solution.py:42
  252.6 5.0 collective-permute-start.13
  256.2 4.3 collective-permute-start.12
  262.8 6.0 %collective-permute-start.14 = (f32[7,2,2,8]{3,2,1,0:T(2,128)S(1)}, f32[7,2,2,8]{3,2,1,0:T(2,128)S(1)}, u32[]{:S(2)}, u32[]{:S(2)}) collective-permute-start(f32[7,2,2,8]{3,2,1,0:T(2,128)S(1)} %fusion.40), channel_id=1, source_target_pairs={{0,4},{1,5},{2,6},{3,7},{4,0},{5,1},{6,2},{7,3},{8,12},{9,13},{10,... | collective-permute-start | bytes 2696 | tf_op jit(solution)/shard_map/ppermute | solution.py:88
  270.7 20.2 %all-to-all-start.8 = ((f32[64,6,16]{2,1,0:T(8,128)}), f32[64,6,16]{2,1,0:T(8,128)S(1)}, u32[]{:S(2)}, u32[]{:S(2)}) async-start(f32[64,6,16]{2,1,0:T(8,128)} %broadcast_in_dim.49), calls=%async_computation.8 | async-start | bytes 524288 | tf_op jit(solution)/shard_map/all_to_all | solution.py:42
  293.3 4.2 collective-permute-start.16
  296.1 4.3 collective-permute-start.15
  300.9 4.4 collective-permute-start.17
  306.3 18.5 %all-to-all-start.9 = ((f32[64,6,4]{1,2,0:T(4,128)}), f32[64,6,4]{1,2,0:T(4,128)S(1)}, u32[]{:S(2)}, u32[]{:S(2)}) async-start(f32[64,6,4]{1,2,0:T(4,128)} %broadcast_in_dim.51), calls=%async_computation.9 | async-start | bytes 262144 | tf_op jit(solution)/shard_map/all_to_all | solution.py:42
  327.2 4.2 collective-permute-start.19
  330.0 4.3 collective-permute-start.18
  335.3 17.2 %all-to-all-start.10 = ((f32[64,6,4]{1,2,0:T(4,128)}), f32[64,6,4]{1,2,0:T(4,128)S(1)}, u32[]{:S(2)}, u32[]{:S(2)}) async-start(f32[64,6,4]{1,2,0:T(4,128)} %broadcast_in_dim.53), calls=%async_computation.10 | async-start | bytes 262144 | tf_op jit(solution)/shard_map/all_to_all | solution.py:42
  355.1 4.2 collective-permute-start.21
  357.9 4.3 collective-permute-start.20
  363.3 19.2 %all-to-all-start.11 = ((f32[64,6,16]{2,1,0:T(8,128)}), f32[64,6,16]{2,1,0:T(8,128)S(1)}, u32[]{:S(2)}, u32[]{:S(2)}) async-start(f32[64,6,16]{2,1,0:T(8,128)} %broadcast_in_dim.57), calls=%async_computation.11 | async-start | bytes 524288 | tf_op jit(solution)/shard_map/all_to_all | solution.py:42
  385.2 4.2 collective-permute-start.23
  388.1 4.3 collective-permute-start.22
  393.5 16.9 %all-to-all-start.12 = ((f32[64,1,384]{2,1,0:T(1,128)}), f32[64,1,384]{2,1,0:T(1,128)S(1)}, u32[]{:S(2)}, u32[]{:S(2)}) async-start(f32[64,1,384]{2,1,0:T(1,128)} %reshape.2552), calls=%async_computation.12 | async-start | bytes 196608 | tf_op jit(solution)/shard_map/all_to_all | solution.py:42
  414.8 4.2 collective-permute-start.25
  417.7 4.3 collective-permute-start.24
  425.0 23.7 %all-to-all-start.13 = ((f32[64,6,256]{2,1,0:T(8,128)}), f32[64,6,256]{2,1,0:T(8,128)S(1)}, u32[]{:S(2)}, u32[]{:S(2)}) async-start(f32[64,6,256]{2,1,0:T(8,128)} %broadcast_in_dim.63), calls=%async_computation.13 | async-start | bytes 1048576 | tf_op jit(solution)/shard_map/all_to_all | solution.py:42
  453.8 0.7 copy-start.34
  468.7 0.7 copy-start.19
  470.5 4.2 collective-permute-start.27
  473.4 4.3 collective-permute-start.26
  520.9 4.3 collective-permute-start.29
  523.8 4.4 collective-permute-start.28
  536.1 13.0 %all-to-all-start.18 = ((f32[32,1,768]{2,1,0:T(1,128)}), f32[32,1,768]{2,1,0:T(1,128)S(1)}, u32[]{:S(2)}, u32[]{:S(2)}) async-start(f32[32,1,768]{2,1,0:T(1,128)} %reshape.2560), calls=%async_computation.18 | async-start | bytes 196608 | tf_op jit(solution)/shard_map/all_to_all | solution.py:30
  555.7 15.2 %all-to-all-start.19 = ((f32[64,1,128]{2,1,0:T(1,128)}), f32[64,1,128]{2,1,0:T(1,128)S(1)}, u32[]{:S(2)}, u32[]{:S(2)}) async-start(f32[64,1,128]{2,1,0:T(1,128)} %reshape.2562), calls=%async_computation.19 | async-start | bytes 65536 | tf_op jit(solution)/shard_map/all_to_all | solution.py:274
  (93 other events, 62.7 us)
